TPU v7x, 128 devices: a whole 4x4x4 slice. The times are simulated.
128 devices in a mesh: group: 4 (over z), member: 32 (over x, y, core).
Axes of the slice: x: 4, y: 4, z: 4, core: 2. Of those that a mesh axis runs over, the one named last changes fastest.
Arguments:
- passage_hidden: bfloat16 [16384, 768], P(('group', 'member')), may hold values from -6 to 6
- query_hidden: bfloat16 [65536, 768], P(('group', 'member')), may hold values from -96 to 96
- proj_weight: bfloat16 [768, 768], replicated, may hold values from -0.21875 to 0.21875
- cluster: int32 [16384], P(('group', 'member')), may hold values from 0 to 3, as said below
- place: int32 [16384], P(('group', 'member')), may hold values from 0 to 4095, as said below
- positive: int32 [65536], P(('group', 'member')), may hold values from 0 to 4095
- loss_weight: float32 [65536], P(('group', 'member')), may hold values from 8 to 64
Outputs:
- loss: float32 [65536], P(('group', 'member'))
- grad_query_hidden: bfloat16 [65536, 768], P(('group', 'member'))
- grad_passage_hidden: bfloat16 [16384, 768], P(('group', 'member'))
- grad_weight: float32 [768, 768], replicated
Inputs may be any that keep to these rules, and one draw needn't show every extreme that they name: Every cluster group holds exactly 4096 passages. Within one cluster group each row 0 to 4095 is taken by exactly one passage. Call the owner of a passage the device cluster * 32 + place // 128; every device owns 128 passages, every device sends at most 2 passages to one owner and exactly 2 to some owner, and the count that device d sends to owner o depends only on o - d modulo 128.
All inputs are finite; a program needn't handle non-finite values.
Results may differ from a plain program's by a relative error of at most 0.0095.
Values may be sent and summed in bfloat16 or wider, within the bound.
No kernel may reach another device: no remote copies, remote signals or barrier semaphores. Data moves between devices by JAX's collectives and lax.ppermute only.
A program may use at most 128 MiB of HBM per device.

v0:
```python
import math

import jax
import jax.numpy as jnp
from jax import lax
from jax.sharding import PartitionSpec as P


MEMBER = ("chip", "core")
ALL = ("group", "chip", "core")


def contract(left, right, left_dim, right_dim):
    return lax.dot_general(
        left, right, (((left_dim,), (right_dim,)), ((), ())), preferred_element_type=jnp.float32
    )


def body(passage_hidden, query_hidden, proj_weight, cluster, place, positive, loss_weight):
    rows, width = passage_hidden.shape
    members = lax.axis_size("chip") * lax.axis_size("core")
    groups = lax.axis_size("group")
    devices = members * groups
    group_rows = rows * members
    capacity = 2 * rows // devices
    factor = 1.0 / math.sqrt(width)
    passage_emb = jnp.dot(passage_hidden, proj_weight, preferred_element_type=jnp.float32).astype(
        jnp.bfloat16
    )
    query_emb = jnp.dot(query_hidden, proj_weight, preferred_element_type=jnp.float32).astype(
        jnp.bfloat16
    )
    target = cluster * group_rows + place
    owner = target // rows
    slot = target % rows
    order = jnp.arange(rows, dtype=jnp.int32)
    earlier_same = (owner[:, None] == owner[None, :]) & (order[:, None] > order[None, :])
    rank = jnp.sum(earlier_same.astype(jnp.int32), axis=1)
    position = owner * capacity + rank
    tag_width = 128
    tag = jnp.broadcast_to(slot.astype(jnp.bfloat16)[:, None], (rows, tag_width))
    both = jnp.concatenate([passage_emb, passage_hidden, tag], axis=1)
    send_rows = jnp.zeros((devices * capacity, 2 * width + tag_width), jnp.bfloat16)
    send_rows = send_rows.at[:, 2 * width :].set(rows).at[position].set(both)
    got = lax.all_to_all(send_rows, ALL, split_axis=0, concat_axis=0, tiled=True)
    got_rows = got[:, : 2 * width]
    got_slots = got[:, 2 * width].astype(jnp.int32)
    relaid = jnp.zeros((rows, 2 * width), jnp.bfloat16).at[got_slots].set(got_rows, mode="drop")
    group_passages = lax.all_gather(relaid[:, :width], MEMBER, axis=0, tiled=True)
    group_hidden = lax.all_gather(relaid[:, width:], MEMBER, axis=0, tiled=True)
    scores = contract(query_emb, group_passages, 1, 1) * factor
    top = jnp.max(scores, axis=1, keepdims=True)
    lse = top[:, 0] + jnp.log(jnp.sum(jnp.exp(scores - top), axis=1))
    hit = jnp.arange(group_rows, dtype=jnp.int32)[None, :] == positive[:, None]
    loss = lse - jnp.sum(jnp.where(hit, scores, 0.0), axis=1)
    coef = (
        loss_weight[:, None] * (jnp.exp(scores - lse[:, None]) - hit.astype(jnp.float32)) * factor
    ).astype(jnp.bfloat16)
    query_grad = jnp.dot(coef, group_passages, preferred_element_type=jnp.float32).astype(
        jnp.bfloat16
    )
    partial = contract(coef, query_emb, 0, 0)
    local_weight = contract(query_hidden, query_grad, 0, 0) + contract(group_hidden, partial, 0, 0)
    weight_rows = width // members
    chips = lax.axis_size("chip")
    core = lax.axis_index("core")
    swap = [(0, 1), (1, 0)]
    weight_split = local_weight.reshape(chips, 2, weight_rows, width)
    weight_kept = jnp.where(core == 0, weight_split[:, 0], weight_split[:, 1])
    weight_given = jnp.where(core == 0, weight_split[:, 1], weight_split[:, 0])
    weight_paired = weight_kept + lax.ppermute(weight_given, "core", swap)
    weight_pieces = lax.all_to_all(weight_paired, "chip", 0, 0, tiled=True)
    weight_share = jnp.sum(weight_pieces, axis=0)
    step = 1
    while step < groups:
        pairs = [(index, index ^ step) for index in range(groups)]
        weight_share = weight_share + lax.ppermute(weight_share, "group", pairs)
        step *= 2
    grad_weight = lax.all_gather(weight_share, MEMBER, axis=0, tiled=True) / devices
    split = partial.reshape(chips, 2, rows, width)
    kept = jnp.where(core == 0, split[:, 0], split[:, 1])
    given = jnp.where(core == 0, split[:, 1], split[:, 0]).astype(jnp.bfloat16)
    paired = kept + lax.ppermute(given, "core", swap).astype(jnp.float32)
    pieces = lax.all_to_all(
        paired.astype(jnp.bfloat16), "chip", split_axis=0, concat_axis=0, tiled=True
    )
    relaid_grad = jnp.sum(pieces.astype(jnp.float32), axis=0).astype(jnp.bfloat16)
    back_rows = relaid_grad[jnp.minimum(got_slots, rows - 1)]
    returned = lax.all_to_all(
        back_rows, ALL, split_axis=0, concat_axis=0, tiled=True
    )
    passage_grad = returned[position]
    grad_passage_hidden = contract(passage_grad, proj_weight, 1, 1).astype(jnp.bfloat16)
    grad_query_hidden = contract(query_grad, proj_weight, 1, 1).astype(jnp.bfloat16)
    return (loss, grad_query_hidden, grad_passage_hidden, grad_weight)


def solution(mesh):
    groups, members = mesh.devices.shape
    mesh = jax.sharding.Mesh(
        mesh.devices.reshape(groups, members // 2, 2), ("group", "chip", "core")
    )
    in_specs = (
        P(("group", "chip", "core"), None),
        P(("group", "chip", "core"), None),
        P(),
        P(("group", "chip", "core")),
        P(("group", "chip", "core")),
        P(("group", "chip", "core")),
        P(("group", "chip", "core")),
    )
    out_specs = (
        P(("group", "chip", "core")),
        P(("group", "chip", "core"), None),
        P(("group", "chip", "core"), None),
        P(),
    )
    return jax.shard_map(body, mesh=mesh, in_specs=in_specs, out_specs=out_specs, check_vma=False)
```

profile of v0, /device:TPU:1, one launch (start us, length us, event | category | flops | bytes accessed | tf_op | source)
XLA Modules:
  0.0 279.9 jit_solution(2270200137131765824)
XLA Ops:
  7.2 0.8 fusion.18
  8.0 0.7 and_select_fusion.1
  8.7 0.2 convert_reduce_fusion
  8.9 1.3 convolution_convert_fusion.4
  10.3 2.1 scatter_custom_fusion
  12.5 0.3 all_to_all.22
  12.8 28.2 %all_to_all.34 = bf16[128,2,1664]{2,1,0:T(2,128)(2,1)} all-to-all(bf16[128,2,1664]{2,1,0:T(2,128)(2,1)S(1)} %all_to_all.22), channel_id=1, replica_groups=mesh['group'=4,'chip'=16,'core'=2] {'group','chip','core'}, dimensions={0} | all-to-all | bytes 1703936 | tf_op jit(solution)/shard_map/all_to_all | solution.py:45
  41.0 2.4 all_to_all.24
  43.4 0.2 fusion.16
  43.6 1.9 scatter_custom_fusion.1
  45.4 0.8 fusion.20
  46.3 0.7 all-gather.6.cloned.1.call-update
  47.0 0.2 all-gather.8.cloned.1.call-start
  47.2 1.9 convolution_convert_fusion.1
  49.1 42.8 %all-gather.4.cloned.1.call-done = bf16[4096,768]{1,0:T(8,128)(2,1)} async-done(((bf16[128,768]{1,0:T(8,128)(2,1)}), bf16[4096,768]{1,0:T(8,128)(2,1)}) %all-gather.4.cloned.1.call-update) | async-done | bytes 6291472 | tf_op jit(solution)/shard_map/all_gather | solution.py:49
  91.9 5.8 %multiply_reduce_fusion = (f32[512]{0:T(512)S(1)}, f32[512,4096]{1,0:T(8,128)S(1)}) fusion(bf16[512,768]{1,0:T(8,128)(2,1)S(1)} %convolution_convert_fusion.1, bf16[4096,768]{1,0:T(8,128)(2,1)} %all-gather.4.cloned.1.call-done), kind=kOutput, calls=%fused_computation.8 | convolution fusion | flops 3225419264 | bytes 15468544 | tf_op jit(solution)/shard_map/dot_general | solution.py:14
  97.7 3.1 %select_reduce_fusion = (f32[512]{0:T(512)S(1)}, f32[512]{0:T(512)S(1)}) fusion(f32[512,4096]{1,0:T(8,128)S(1)} %get-tuple-element.27, s32[512]{0:T(512)S(1)} %copy-done.3, f32[512]{0:T(512)S(1)} %get-tuple-element.26), kind=kLoop, calls=%fused_computation.5 | loop fusion | flops 12581888 | bytes 8396800 | tf_op jit(solution)/shard_map/reduce_sum | solution.py:55
  100.8 0.6 fusion.19
  101.4 3.9 %multiply_convert_fusion = bf16[512,4096]{1,0:T(8,128)(2,1)S(1)} fusion(f32[512,4096]{1,0:T(8,128)S(1)} %get-tuple-element.27, f32[512]{0:T(512)S(1)} %get-tuple-element.21, f32[512]{0:T(512)S(1)} %copy-done.4, s32[512]{0:T(512)S(1)} %copy-done.3), kind=kLoop, calls=%fused_computation.4 | loop fusion | flops 16777216 | bytes 12589056 | tf_op jit(solution)/shard_map/convert_element_type | solution.py:58
  105.3 3.6 %fusion.21 = f32[4096,768]{1,0:T(8,128)S(1)} fusion(bf16[512,4096]{1,0:T(8,128)(2,1)S(1)} %multiply_convert_fusion, bf16[512,768]{1,0:T(8,128)(2,1)S(1)} %convolution_convert_fusion.1), kind=kOutput, calls=%fused_computation.56 | convolution fusion | flops 3221225472 | bytes 17563648 | tf_op jit(solution)/shard_map/dot_general | solution.py:14
  109.0 4.6 %copy-done.1 = f32[4096,768]{1,0:T(8,128)} copy-done((f32[4096,768]{1,0:T(8,128)}, f32[4096,768]{1,0:T(8,128)S(1)}, u32[]{:S(2)}) %copy-start.1) | copy-done | bytes 12582936
  113.5 2.3 fusion.3
  115.8 0.3 collective-permute-start
  116.1 5.6 %convolution_convert_fusion.2 = bf16[512,768]{1,0:T(8,128)(2,1)S(1)} fusion(bf16[512,4096]{1,0:T(8,128)(2,1)S(1)} %multiply_convert_fusion, bf16[4096,768]{1,0:T(8,128)(2,1)} %all-gather.4.cloned.1.call-done), kind=kOutput, calls=%fused_computation.18 | convolution fusion | flops 3221618688 | bytes 11272192 | tf_op jit(solution)/shard_map/dot_general | solution.py:59
  121.7 20.7 %all-gather.6.cloned.1.call-done = bf16[4096,768]{1,0:T(8,128)(2,1)} async-done(((bf16[128,768]{1,0:T(8,128)(2,1)}), bf16[4096,768]{1,0:T(8,128)(2,1)}) %all-gather.6.cloned.1.call-update) | async-done | bytes 6291472 | tf_op jit(solution)/shard_map/all_gather | solution.py:50
  142.4 10.1 %fusion.22 = f32[768,768]{1,0:T(8,128)S(1)} fusion(bf16[4096,768]{1,0:T(8,128)(2,1)} %all-gather.6.cloned.1.call-done, f32[4096,768]{1,0:T(8,128)} %copy-done.1), kind=kOutput, calls=%fused_computation.57 | convolution fusion | flops 4831838208 | bytes 21233664 | tf_op jit(solution)/shard_map/dot_general | solution.py:14
  152.5 0.9 bitcast_add_fusion
  153.6 0.4 collective-permute-start.1
  154.0 2.6 collective-permute-done.1
  156.5 0.2 fusion.5
  156.7 21.6 %all_to_all.35 = f32[16,24,768]{2,1,0:T(8,128)S(1)} all-to-all(f32[16,24,768]{2,1,0:T(8,128)S(1)} %fusion.5), channel_id=1, replica_groups=mesh['group'=4,'chip'=16,'core'=2] {'chip'}, dimensions={0} | all-to-all | bytes 2359296 | tf_op jit(solution)/shard_map/all_to_all | solution.py:72
  178.4 1.3 collective-permute-start.2
  179.8 1.9 collective-permute-done.2
  181.7 2.9 %collective-permute-start.3 = (f32[24,768]{1,0:T(8,128)S(1)}, f32[24,768]{1,0:T(8,128)S(1)}, u32[]{:S(2)}, u32[]{:S(2)}) collective-permute-start(f32[24,768]{1,0:T(8,128)S(1)} %add.61), channel_id=1, source_target_pairs={{0,64},{32,96},{64,0},{96,32},{1,65},{33,97},{65,1},{97,33},{2,66}... | collective-permute-start | bytes 221192 | tf_op jit(solution)/shard_map/ppermute | solution.py:77
  184.7 2.3 collective-permute-done.3
  186.9 0.6 add.62
  187.6 8.6 %fusion.2 = bf16[16,128,768]{2,1,0:T(8,128)(2,1)} fusion(bf16[16,128,768]{2,1,0:T(8,128)(2,1)} %collective-permute-done, f32[16,2,128,768]{3,2,1,0:T(8,128)} %bitcast.65, pred[]{:T(512)S(6)} %eq.40), kind=kLoop, calls=%fused_computation.12 | loop fusion | flops 6291456 | bytes 18874368 | tf_op jit(solution)/shard_map/convert_element_type | solution.py:85
  196.2 4.5 %all-to-all-start.1 = ((bf16[16,128,768]{2,1,0:T(8,128)(2,1)}), bf16[16,128,768]{2,1,0:T(8,128)(2,1)}, u32[]{:S(2)}, u32[]{:S(2)}) async-start(bf16[16,128,768]{2,1,0:T(8,128)(2,1)} %fusion.2), calls=%async_computation.1 | async-start | bytes 6291456 | tf_op jit(solution)/shard_map/all_to_all | solution.py:84
  200.7 36.8 %all-to-all-done.1 = bf16[16,128,768]{2,1,0:T(8,128)(2,1)} async-done(((bf16[16,128,768]{2,1,0:T(8,128)(2,1)}), bf16[16,128,768]{2,1,0:T(8,128)(2,1)}, u32[]{:S(2)}, u32[]{:S(2)}) %all-to-all-start.1) | async-done | bytes 3145760 | tf_op jit(solution)/shard_map/all_to_all | solution.py:84
  237.5 2.3 reduce_sum.51
  239.8 1.2 gather_fusion
  241.0 0.9 all_to_all.26
  241.9 13.8 %all-to-all-start.2 = ((bf16[128,2,768]{2,1,0:T(2,128)(2,1)}), bf16[128,2,768]{2,1,0:T(2,128)(2,1)S(1)}, u32[]{:S(2)}, u32[]{:S(2)}) async-start(bf16[128,2,768]{2,1,0:T(2,128)(2,1)} %all_to_all.26), calls=%async_computation.2 | async-start | bytes 786432 | tf_op jit(solution)/shard_map/all_to_all | solution.py:89
  255.7 1.7 convolution_convert_fusion
  257.4 10.5 %all-to-all-done.2 = bf16[128,2,768]{2,1,0:T(2,128)(2,1)S(1)} async-done(((bf16[128,2,768]{2,1,0:T(2,128)(2,1)}), bf16[128,2,768]{2,1,0:T(2,128)(2,1)S(1)}, u32[]{:S(2)}, u32[]{:S(2)}) %all-to-all-start.2) | async-done | bytes 393248 | tf_op jit(solution)/shard_map/all_to_all | solution.py:89
  268.0 0.9 gather_fusion.1
  268.9 1.2 convolution_convert_fusion.3
  270.1 3.2 %broadcast_multiply_fusion = f32[768,768]{1,0:T(8,128)} fusion(f32[768,768]{1,0:T(8,128)} %all-gather.8.cloned.1.call-done), kind=kLoop, calls=%fused_computation.22 | loop fusion | flops 589824 | bytes 4718592 | tf_op jit(solution)/shard_map/div | solution.py:79
  (26 shorter events, 0.7 us)
Async XLA Ops:
  7.2 1.7 copy-start
  7.2 84.7 %all-gather.4.cloned.1.call-start = ((), (), s32[]{:S(2)}) async-start(), calls=%async_computation.4 | async-start | bytes 6488064 | tf_op jit(solution)/shard_map/all_gather | solution.py:49
  46.2 96.2 %all-gather.6.cloned.1.call-start = ((), (), s32[]{:S(2)}) async-start(), calls=%async_computation.5 | async-start | bytes 6488064 | tf_op jit(solution)/shard_map/all_gather | solution.py:50
  47.0 223.2 %all-gather.8.cloned.1.call-start = ((), (), s32[]{:S(2)}) async-start(), calls=%async_computation.6 | async-start | bytes 2433024 | tf_op jit(solution)/shard_map/all_gather | solution.py:79
  49.1 48.6 %copy-start.3 = (s32[512]{0:T(512)S(1)}, s32[512]{0:T(512)}, u32[]{:S(2)}) copy-start(s32[512]{0:T(512)} %param.14) | copy-start | bytes 6148
  97.7 3.7 %copy-start.4 = (f32[512]{0:T(512)S(1)}, f32[512]{0:T(512)}, u32[]{:S(2)}) copy-start(f32[512]{0:T(512)} %param.15) | copy-start | bytes 6148
  109.0 4.6 %copy-start.1 = (f32[4096,768]{1,0:T(8,128)}, f32[4096,768]{1,0:T(8,128)S(1)}, u32[]{:S(2)}) copy-start(f32[4096,768]{1,0:T(8,128)S(1)} %fusion.21) | copy-start | bytes 37748740
  115.8 71.8 %collective-permute-start = (bf16[16,128,768]{2,1,0:T(8,128)(2,1)}, bf16[16,128,768]{2,1,0:T(8,128)(2,1)}, u32[]{:S(2)}, u32[]{:S(2)}) collective-permute-start(bf16[16,128,768]{2,1,0:T(8,128)(2,1)} %fusion.3), channel_id=1, source_target_pairs={{0,1},{1,0},{2,3},{3,2},{4,5},{5,4},{6,7},{7,6},{8,9},{9,8},{10,11... | collective-permute-start | bytes 9437192 | tf_op jit(solution)/shard_map/ppermute | solution.py:83
  121.7 30.8 %copy-start.2 = (bf16[512,768]{1,0:T(8,128)(2,1)S(1)}, bf16[512,768]{1,0:T(8,128)(2,1)}, u32[]{:S(2)}) copy-start(bf16[512,768]{1,0:T(8,128)(2,1)} %param.10) | copy-start | bytes 2359300
  153.6 2.9 %collective-permute-start.1 = (f32[16,24,768]{2,1,0:T(8,128)S(1)}, f32[16,24,768]{2,1,0:T(8,128)S(1)}, u32[]{:S(2)}, u32[]{:S(2)}) collective-permute-start(f32[16,24,768]{2,1,0:T(8,128)S(1)} %select_bitcast_fusion), channel_id=1, source_target_pairs={{0,1},{1,0},{2,3},{3,2},{4,5},{5,4},{6,7},{7,6},{8,9},{9,8},{10,11... | collective-permute-start | bytes 3538952 | tf_op jit(solution)/shard_map/ppermute | solution.py:71
  178.4 3.3 %collective-permute-start.2 = (f32[24,768]{1,0:T(8,128)S(1)}, f32[24,768]{1,0:T(8,128)S(1)}, u32[]{:S(2)}, u32[]{:S(2)}) collective-permute-start(f32[24,768]{1,0:T(8,128)S(1)} %reduce_sum.52), channel_id=1, source_target_pairs={{0,32},{32,0},{64,96},{96,64},{1,33},{33,1},{65,97},{97,65},{2,34}... | collective-permute-start | bytes 221192 | tf_op jit(solution)/shard_map/ppermute | solution.py:77
  181.7 5.2 %collective-permute-start.3 = (f32[24,768]{1,0:T(8,128)S(1)}, f32[24,768]{1,0:T(8,128)S(1)}, u32[]{:S(2)}, u32[]{:S(2)}) collective-permute-start(f32[24,768]{1,0:T(8,128)S(1)} %add.61), channel_id=1, source_target_pairs={{0,64},{32,96},{64,0},{96,32},{1,65},{33,97},{65,1},{97,33},{2,66}... | collective-permute-start | bytes 221192 | tf_op jit(solution)/shard_map/ppermute | solution.py:77
  196.2 41.3 %all-to-all-start.1 = ((bf16[16,128,768]{2,1,0:T(8,128)(2,1)}), bf16[16,128,768]{2,1,0:T(8,128)(2,1)}, u32[]{:S(2)}, u32[]{:S(2)}) async-start(bf16[16,128,768]{2,1,0:T(8,128)(2,1)} %fusion.2), calls=%async_computation.1 | async-start | bytes 6291456 | tf_op jit(solution)/shard_map/all_to_all | solution.py:84
  241.9 26.0 %all-to-all-start.2 = ((bf16[128,2,768]{2,1,0:T(2,128)(2,1)}), bf16[128,2,768]{2,1,0:T(2,128)(2,1)S(1)}, u32[]{:S(2)}, u32[]{:S(2)}) async-start(bf16[128,2,768]{2,1,0:T(2,128)(2,1)} %all_to_all.26), calls=%async_computation.2 | async-start | bytes 786432 | tf_op jit(solution)/shard_map/all_to_all | solution.py:89
Sparse Core Ops, SparseCore 0:
  46.3 45.5 all-gather.3
  94.7 47.6 all-gather.5
  187.7 66.9 all-gather.7
where the time goes:
time: 280 us
  waiting for transfers between devices  118 us (42%)
  blocking collectives  49.9 us (18%)
  matrix products  32.1 us (11%)
  other arithmetic  29 us (10%)
  starting transfers between devices  23.5 us (8%)
  between operations  14 us (5%)
  local copies, waits for them, and re-layouts  13.1 us (5%)
    all_gather x1, waiting for transfers between devices, body(): lax.all_gather(relaid[:, :width], MEMBER, axis=0, tiled=True)  42.8 us
    all_to_all x1, waiting for transfers between devices, body(): lax.all_to_all(paired.astype(jnp.bfloat16), 'chip', split_axis=0, concat_...  36.8 us
    all_to_all x1, blocking collectives, body(): lax.all_to_all(send_rows, ALL, split_axis=0, concat_axis=0, tiled=True)  28.2 us
    dot_general x6, matrix products, contract(): lax.dot_general(left, right, (((left_dim,), (right_dim,)), ((), ())), pre...  23.3 us
    all_to_all x1, blocking collectives, body(): weight_pieces = lax.all_to_all(weight_paired, 'chip', 0, 0, tiled=True)  21.6 us
    all_gather x1, waiting for transfers between devices, body(): group_hidden = lax.all_gather(relaid[:, width:], MEMBER, axis=0, tiled=True)  20.7 us
    all_to_all x1, starting transfers between devices, body(): lax.all_to_all(back_rows, ALL, split_axis=0, concat_axis=0, tiled=True)  13.8 us
    all_to_all x1, waiting for transfers between devices, body(): lax.all_to_all(back_rows, ALL, split_axis=0, concat_axis=0, tiled=True)  10.5 us
  transfers between devices with their start and end apart: 9, of which 7 were waited for; matrix products, arithmetic and copies ran while one was open for 20% of the time, Pallas kernels for 0%

commit v1 on v0

--- a/solution.py
+++ b/solution.py
@@ -46,8 +46,9 @@
     got_rows = got[:, : 2 * width]
     got_slots = got[:, 2 * width].astype(jnp.int32)
     relaid = jnp.zeros((rows, 2 * width), jnp.bfloat16).at[got_slots].set(got_rows, mode="drop")
-    group_passages = lax.all_gather(relaid[:, :width], MEMBER, axis=0, tiled=True)
-    group_hidden = lax.all_gather(relaid[:, width:], MEMBER, axis=0, tiled=True)
+    group_both = lax.all_gather(relaid, MEMBER, axis=0, tiled=True)
+    group_passages = group_both[:, :width]
+    group_hidden = group_both[:, width:]
     scores = contract(query_emb, group_passages, 1, 1) * factor
     top = jnp.max(scores, axis=1, keepdims=True)
     lse = top[:, 0] + jnp.log(jnp.sum(jnp.exp(scores - top), axis=1))
@@ -59,11 +60,27 @@
     query_grad = jnp.dot(coef, group_passages, preferred_element_type=jnp.float32).astype(
         jnp.bfloat16
     )
-    partial = contract(coef, query_emb, 0, 0)
-    local_weight = contract(query_hidden, query_grad, 0, 0) + contract(group_hidden, partial, 0, 0)
+    chips = members // 2
+    core = lax.axis_index("core")
+    coef_split = coef.reshape(-1, chips, 2, rows)
+    hidden_split = group_hidden.reshape(chips, 2, rows, width)
+    own_coef = lax.dynamic_index_in_dim(coef_split, core, axis=2, keepdims=False)
+    other_coef = lax.dynamic_index_in_dim(coef_split, 1 - core, axis=2, keepdims=False)
+    own_hidden = lax.dynamic_index_in_dim(hidden_split, core, axis=1, keepdims=False)
+    other_hidden = lax.dynamic_index_in_dim(hidden_split, 1 - core, axis=1, keepdims=False)
+    kept = lax.dot_general(
+        own_coef, query_emb, (((0,), (0,)), ((), ())), preferred_element_type=jnp.float32
+    )
+    other = lax.dot_general(
+        other_coef, query_emb, (((0,), (0,)), ((), ())), preferred_element_type=jnp.float32
+    )
+    passage_term = lax.dot_general(
+        own_hidden, kept, (((0, 1), (0, 1)), ((), ())), preferred_element_type=jnp.float32
+    ) + lax.dot_general(
+        other_hidden, other, (((0, 1), (0, 1)), ((), ())), preferred_element_type=jnp.float32
+    )
+    local_weight = contract(query_hidden, query_grad, 0, 0) + passage_term
     weight_rows = width // members
-    chips = lax.axis_size("chip")
-    core = lax.axis_index("core")
     swap = [(0, 1), (1, 0)]
     weight_split = local_weight.reshape(chips, 2, weight_rows, width)
     weight_kept = jnp.where(core == 0, weight_split[:, 0], weight_split[:, 1])
@@ -76,10 +93,8 @@
         pairs = [(index, index ^ step) for index in range(groups)]
         weight_share = weight_share + lax.ppermute(weight_share, "group", pairs)
         step *= 2
-    grad_weight = lax.all_gather(weight_share, MEMBER, axis=0, tiled=True) / devices
-    split = partial.reshape(chips, 2, rows, width)
-    kept = jnp.where(core == 0, split[:, 0], split[:, 1])
-    given = jnp.where(core == 0, split[:, 1], split[:, 0]).astype(jnp.bfloat16)
+    grad_weight = lax.all_gather(weight_share / devices, MEMBER, axis=0, tiled=True)
+    given = other.astype(jnp.bfloat16)
     paired = kept + lax.ppermute(given, "core", swap).astype(jnp.float32)
     pieces = lax.all_to_all(
         paired.astype(jnp.bfloat16), "chip", split_axis=0, concat_axis=0, tiled=True

time: 280 us -> 307 us (1.096)
  local copies, waits for them, and re-layouts: 13.1 us -> 52.7 us
  other arithmetic: 29 us -> 16.2 us
  waiting for transfers between devices: 118 us -> 113 us
    dynamic_slice x0 -> x3, local copies, waits for them, and re-layouts: none -> 29.2 us  [the longest x2 20.2 us: body(): lax.dynamic_index_in_dim(coef_split, 1 - core, axis=2, keepdims=False)]
    dot_general x0 -> x4, matrix products: none -> 17.6 us  [the longest x1 5.34 us: body(): lax.dot_general(own_coef, query_emb, (((0,), (0,)), ((), ())), preferred_...]
    dot_general x6 -> x4, matrix products: 23.3 us -> 9.48 us  [contract(): lax.dot_general(left, right, (((left_dim,), (right_dim,)), ((), ())), pre...]
    convert_element_type x2 -> x0, other arithmetic: 10.9 us -> none  [the longest x1 8.61 us: body(): paired.astype(jnp.bfloat16)]
    reshape x0 -> x1, local copies, waits for them, and re-layouts: none -> 7.74 us  [body(): coef_split = coef.reshape(-1, chips, 2, rows)]
    all_gather x3 -> x2, waiting for transfers between devices: 63.5 us -> 58.5 us  [the longest x1 58.5 us: body(): group_both = lax.all_gather(relaid, MEMBER, axis=0, tiled=True)]
  transfers between devices with their start and end apart: 9 -> 8, of which waited for: 7 -> 6; matrix products, arithmetic and copies ran while one was open for 20% -> 10% of each run, Pallas kernels for 0% -> 0%
where the time goes in v1:
time: 307 us; the launch traced here: 306 us
  waiting for transfers between devices  113 us (37%)
  local copies, waits for them, and re-layouts  52.7 us (17%)
  blocking collectives  50.6 us (16%)
  matrix products  34.8 us (11%)
  starting transfers between devices  23.4 us (8%)
  other arithmetic  16.2 us (5%)
  between operations  14.4 us (5%)
    all_gather x1, waiting for transfers between devices, body(): group_both = lax.all_gather(relaid, MEMBER, axis=0, tiled=True)  58.5 us
    all_to_all x1, waiting for transfers between devices, body(): lax.all_to_all(paired.astype(jnp.bfloat16), 'chip', split_axis=0, concat_...  36.4 us
    all_to_all x1, blocking collectives, body(): lax.all_to_all(send_rows, ALL, split_axis=0, concat_axis=0, tiled=True)  28.2 us
    all_to_all x1, blocking collectives, body(): weight_pieces = lax.all_to_all(weight_paired, 'chip', 0, 0, tiled=True)  22.4 us
    dynamic_slice x2, local copies, waits for them, and re-layouts, body(): lax.dynamic_index_in_dim(coef_split, 1 - core, axis=2, keepdims=False)  20.2 us
    all_to_all x1, starting transfers between devices, body(): lax.all_to_all(back_rows, ALL, split_axis=0, concat_axis=0, tiled=True)  13.5 us
    all_to_all x1, waiting for transfers between devices, body(): lax.all_to_all(back_rows, ALL, split_axis=0, concat_axis=0, tiled=True)  11.6 us
    dot_general x4, matrix products, contract(): lax.dot_general(left, right, (((left_dim,), (right_dim,)), ((), ())), pre...  9.48 us
  transfers between devices with their start and end apart: 8, of which 6 were waited for; matrix products, arithmetic and copies ran while one was open for 10% of the time, Pallas kernels for 0%

profile of v1, /device:TPU:1, one launch (start us, length us, event | category | flops | bytes accessed | tf_op | source)
XLA Modules:
  0.0 305.6 jit_solution(15380365847520930645)
XLA Ops:
  7.2 0.8 fusion.38
  8.0 0.7 and_select_fusion.1
  8.9 1.3 convolution_convert_fusion.3
  10.3 2.1 scatter_custom_fusion
  12.5 0.3 all_to_all.22
  12.8 28.2 %all_to_all.34 = bf16[128,2,1664]{2,1,0:T(2,128)(2,1)} all-to-all(bf16[128,2,1664]{2,1,0:T(2,128)(2,1)S(1)} %all_to_all.22), channel_id=1, replica_groups=mesh['group'=4,'chip'=16,'core'=2] {'group','chip','core'}, dimensions={0} | all-to-all | bytes 1703936 | tf_op jit(solution)/shard_map/all_to_all | solution.py:45
  41.0 2.4 all_to_all.24
  43.6 2.5 scatter_custom_fusion.1
  46.1 0.2 all-gather.5.cloned.1.call-start
  46.4 0.8 convolution_convert_fusion.1
  47.2 58.5 %all-gather.3.cloned.1.call-done = bf16[4096,1536]{1,0:T(8,128)(2,1)} async-done(((bf16[128,1536]{1,0:T(8,128)(2,1)}), bf16[4096,1536]{1,0:T(8,128)(2,1)}) %all-gather.3.cloned.1.call-update) | async-done | bytes 12582928 | tf_op jit(solution)/shard_map/all_gather | solution.py:49
  105.7 5.7 %multiply_reduce_fusion = (f32[512]{0:T(512)S(1)}, f32[512,4096]{1,0:T(8,128)S(1)}) fusion(bf16[512,768]{1,0:T(8,128)(2,1)S(1)} %convolution_convert_fusion.1, bf16[4096,1536]{1,0:T(8,128)(2,1)} %all-gather.3.cloned.1.call-done), kind=kOutput, calls=%fused_computation.8 | convolution fusion | flops 3225419264 | bytes 15468544 | tf_op jit(solution)/shard_map/dot_general | solution.py:14
  111.5 3.1 %select_reduce_fusion = (f32[512]{0:T(512)S(1)}, f32[512]{0:T(512)S(1)}) fusion(f32[512,4096]{1,0:T(8,128)S(1)} %get-tuple-element.27, s32[512]{0:T(512)S(1)} %copy-done.8, f32[512]{0:T(512)S(1)} %get-tuple-element.26), kind=kLoop, calls=%fused_computation.5 | loop fusion | flops 12581888 | bytes 8396800 | tf_op jit(solution)/shard_map/reduce_sum | solution.py:56
  114.6 0.6 fusion.39
  115.2 5.2 %multiply_convert_fusion = bf16[512,4096]{1,0:T(8,128)(2,1)} fusion(f32[512,4096]{1,0:T(8,128)S(1)} %get-tuple-element.27, f32[512]{0:T(512)S(1)} %get-tuple-element.21, f32[512]{0:T(512)S(1)} %copy-done.9, s32[512]{0:T(512)S(1)} %copy-done.8), kind=kLoop, calls=%fused_computation.4 | loop fusion | flops 16777216 | bytes 12589056 | tf_op jit(solution)/shard_map/convert_element_type | solution.py:59
  120.4 7.7 %reshape.61 = bf16[512,16,2,128]{3,2,1,0:T(2,128)(2,1)} reshape(bf16[512,4096]{1,0:T(8,128)(2,1)} %multiply_convert_fusion) | data formatting | bytes 8388608 | tf_op jit(solution)/shard_map/reshape | solution.py:65
  128.1 11.3 %constant_dynamic-slice_fusion = (bf16[512,16,1,128]{3,2,1,0:T(2,128)(2,1)}, bf16[512,16,1,128]{3,2,1,0:T(2,128)(2,1)}) fusion(bf16[512,16,2,128]{3,2,1,0:T(2,128)(2,1)} %reshape.61, s32[]{:T(128)S(6)} %select_n.62, s32[]{:T(128)S(6)} %select_n.61), kind=kLoop, calls=%fused_computation.66 | loop fusion | bytes 8388616 | tf_op jit(solution)/shard_map/jit(dynamic_index_in_dim)/dynamic_slice | solution.py:68
  139.4 9.0 %copy.26 = bf16[512,16,1,128]{0,3,1,2:T(8,128)(2,1)S(1)} copy(bf16[512,16,1,128]{3,2,1,0:T(2,128)(2,1)} %get-tuple-element.24) | data formatting | bytes 4194304 | tf_op jit(solution)/shard_map/jit(dynamic_index_in_dim)/dynamic_slice | solution.py:68
  148.4 4.6 %fusion.11 = bf16[16,128,768]{2,1,0:T(8,128)(2,1)} fusion(bf16[512,16,1,128]{0,3,1,2:T(8,128)(2,1)S(1)} %copy.26, bf16[512,768]{1,0:T(8,128)(2,1)} %copy-done.4), kind=kOutput, calls=%fused_computation.22 | convolution fusion | flops 1610612736 | bytes 6029312 | tf_op jit(solution)/shard_map/dot_general | solution.py:74
  153.0 0.3 collective-permute-start
  153.3 9.0 %copy.25 = bf16[512,16,1,128]{0,3,1,2:T(8,128)(2,1)S(1)} copy(bf16[512,16,1,128]{3,2,1,0:T(2,128)(2,1)} %get-tuple-element.25) | data formatting | bytes 4194304 | tf_op jit(solution)/shard_map/jit(dynamic_index_in_dim)/dynamic_slice | solution.py:67
  162.2 3.3 %slice.49 = bf16[4096,768]{1,0:T(8,128)(2,1)S(1)} slice(bf16[4096,1536]{1,0:T(8,128)(2,1)} %all-gather.3.cloned.1.call-done), slice={[0:4096], [768:1536]} | slice | bytes 12582912 | tf_op jit(solution)/shard_map/slice | solution.py:51
  165.6 0.6 copy-done.1
  166.2 5.7 %fusion.17 = bf16[512,768]{1,0:T(8,128)(2,1)S(1)} fusion(bf16[512,4096]{1,0:T(8,128)(2,1)S(1)} %copy-done.1, bf16[4096,1536]{1,0:T(8,128)(2,1)} %all-gather.3.cloned.1.call-done), kind=kOutput, calls=%fused_computation.28 | convolution fusion | flops 3221618688 | bytes 11272192 | tf_op jit(solution)/shard_map/dot_general | solution.py:60
  172.0 0.8 fusion.40
  172.8 4.7 %fusion.4 = f32[768,768,1]{1,0,2:T(8,128)S(1)} fusion(bf16[16,128,768]{2,1,0:T(8,128)(2,1)} %fusion.11, bf16[16,2,128,768]{3,2,1,0:T(8,128)(2,1)S(1)} %bitcast.69, s32[]{:T(128)S(6)} %select_n.62), kind=kOutput, calls=%fused_computation.14 | convolution fusion | flops 2415919104 | bytes 8650756 | tf_op jit(solution)/shard_map/dot_general | solution.py:79
  177.6 5.3 %add_convert_fusion = (bf16[16,128,768]{2,1,0:T(8,128)(2,1)}, bf16[16,128,768]{2,1,0:T(8,128)(2,1)S(1)}) fusion(bf16[16,128,768]{2,1,0:T(8,128)(2,1)} %collective-permute-done, bf16[512,768]{1,0:T(8,128)(2,1)S(1)} %copy-done.5, bf16[512,16,1,128]{0,3,1,2:T(8,128)(2,1)S(1)} %copy.25), kind=kOutput, calls=%fused_computation.9 | convolution fusion | flops 1616904192 | bytes 12320768 | tf_op jit(solution)/shard_map/dot_general | solution.py:71
  182.9 2.9 fusion.10
  186.0 0.3 collective-permute-start.1
  186.3 2.6 collective-permute-done.1
  188.9 0.2 fusion.21
  189.1 22.4 %all_to_all.35 = f32[16,24,768]{2,1,0:T(8,128)S(1)} all-to-all(f32[16,24,768]{2,1,0:T(8,128)S(1)} %fusion.21), channel_id=1, replica_groups=mesh['group'=4,'chip'=16,'core'=2] {'chip'}, dimensions={0} | all-to-all | bytes 2359296 | tf_op jit(solution)/shard_map/all_to_all | solution.py:89
  211.6 1.4 collective-permute-start.2
  212.9 1.9 collective-permute-done.2
  214.9 3.0 collective-permute-start.3
  217.8 2.2 collective-permute-done.3
  220.1 0.6 add_multiply_fusion
  220.7 4.8 %all-to-all-start.1 = ((bf16[16,128,768]{2,1,0:T(8,128)(2,1)}), bf16[16,128,768]{2,1,0:T(8,128)(2,1)}, u32[]{:S(2)}, u32[]{:S(2)}) async-start(bf16[16,128,768]{2,1,0:T(8,128)(2,1)} %get-tuple-element.28), calls=%async_computation.1 | async-start | bytes 6291456 | tf_op jit(solution)/shard_map/all_to_all | solution.py:99
  225.5 36.4 %all-to-all-done.1 = bf16[16,128,768]{2,1,0:T(8,128)(2,1)} async-done(((bf16[16,128,768]{2,1,0:T(8,128)(2,1)}), bf16[16,128,768]{2,1,0:T(8,128)(2,1)}, u32[]{:S(2)}, u32[]{:S(2)}) %all-to-all-start.1) | async-done | bytes 3145760 | tf_op jit(solution)/shard_map/all_to_all | solution.py:99
  261.9 2.3 reduce_sum.51
  264.3 1.2 gather_fusion
  265.5 0.9 all_to_all.26
  266.4 13.5 %all-to-all-start.2 = ((bf16[128,2,768]{2,1,0:T(2,128)(2,1)}), bf16[128,2,768]{2,1,0:T(2,128)(2,1)S(1)}, u32[]{:S(2)}, u32[]{:S(2)}) async-start(bf16[128,2,768]{2,1,0:T(2,128)(2,1)} %all_to_all.26), calls=%async_computation.2 | async-start | bytes 786432 | tf_op jit(solution)/shard_map/all_to_all | solution.py:104
  279.9 1.7 convolution_convert_fusion
  281.6 11.6 %all-to-all-done.2 = bf16[128,2,768]{2,1,0:T(2,128)(2,1)S(1)} async-done(((bf16[128,2,768]{2,1,0:T(2,128)(2,1)}), bf16[128,2,768]{2,1,0:T(2,128)(2,1)S(1)}, u32[]{:S(2)}, u32[]{:S(2)}) %all-to-all-start.2) | async-done | bytes 393248 | tf_op jit(solution)/shard_map/all_to_all | solution.py:104
  293.4 0.9 gather_fusion.1
  294.3 1.2 convolution_convert_fusion.2
  295.5 3.2 %copy.36 = f32[768,768]{1,0:T(8,128)} copy(f32[768,768]{1,0:T(8,128)} %all-gather.5.cloned.1.call-done) | data formatting | bytes 4718592
  (37 shorter events, 1.0 us)
Async XLA Ops:
  7.2 1.7 copy-start
  7.2 98.5 %all-gather.3.cloned.1.call-start = ((), (), s32[]{:S(2)}) async-start(), calls=%async_computation.4 | async-start | bytes 12976128 | tf_op jit(solution)/shard_map/all_gather | solution.py:49
  41.0 5.3 %copy-start.6 = (bf16[512,768]{1,0:T(8,128)(2,1)S(1)}, bf16[512,768]{1,0:T(8,128)(2,1)}, u32[]{:S(2)}) copy-start(bf16[512,768]{1,0:T(8,128)(2,1)} %param.10) | copy-start | bytes 2359300
  46.1 249.4 %all-gather.5.cloned.1.call-start = ((), (), s32[]{:S(2)}) async-start(), calls=%async_computation.5 | async-start | bytes 2433024 | tf_op jit(solution)/shard_map/all_gather | solution.py:96
  47.2 64.3 %copy-start.4 = (bf16[512,768]{1,0:T(8,128)(2,1)}, bf16[512,768]{1,0:T(8,128)(2,1)S(1)}, u32[]{:S(2)}) copy-start(bf16[512,768]{1,0:T(8,128)(2,1)S(1)} %convolution_convert_fusion.1) | copy-start | bytes 2359300
  47.2 64.3 %copy-start.8 = (s32[512]{0:T(512)S(1)}, s32[512]{0:T(512)}, u32[]{:S(2)}) copy-start(s32[512]{0:T(512)} %param.14) | copy-start | bytes 6148
  111.5 3.7 %copy-start.9 = (f32[512]{0:T(512)S(1)}, f32[512]{0:T(512)}, u32[]{:S(2)}) copy-start(f32[512]{0:T(512)} %param.15) | copy-start | bytes 6148
  153.0 24.6 %collective-permute-start = (bf16[16,128,768]{2,1,0:T(8,128)(2,1)}, bf16[16,128,768]{2,1,0:T(8,128)(2,1)}, u32[]{:S(2)}, u32[]{:S(2)}) collective-permute-start(bf16[16,128,768]{2,1,0:T(8,128)(2,1)} %fusion.11), channel_id=1, source_target_pairs={{0,1},{1,0},{2,3},{3,2},{4,5},{5,4},{6,7},{7,6},{8,9},{9,8},{10,11... | collective-permute-start | bytes 9437192 | tf_op jit(solution)/shard_map/ppermute | solution.py:98
  162.2 4.0 %copy-start.1 = (bf16[512,4096]{1,0:T(8,128)(2,1)S(1)}, bf16[512,4096]{1,0:T(8,128)(2,1)}, u32[]{:S(2)}) copy-start(bf16[512,4096]{1,0:T(8,128)(2,1)} %multiply_convert_fusion) | copy-start | bytes 12582916
  166.2 5.7 %copy-start.7 = (bf16[512,768]{1,0:T(8,128)(2,1)S(1)}, bf16[512,768]{1,0:T(8,128)(2,1)}, u32[]{:S(2)}) copy-start(bf16[512,768]{1,0:T(8,128)(2,1)} %param.10) | copy-start | bytes 2359300
  172.0 0.9 copy-start.2
  172.8 4.7 %copy-start.5 = (bf16[512,768]{1,0:T(8,128)(2,1)S(1)}, bf16[512,768]{1,0:T(8,128)(2,1)}, u32[]{:S(2)}) copy-start(bf16[512,768]{1,0:T(8,128)(2,1)} %copy-done.4) | copy-start | bytes 2359300
  186.0 2.9 collective-permute-start.1
  211.6 3.3 %collective-permute-start.2 = (f32[24,768]{1,0:T(8,128)S(1)}, f32[24,768]{1,0:T(8,128)S(1)}, u32[]{:S(2)}, u32[]{:S(2)}) collective-permute-start(f32[24,768]{1,0:T(8,128)S(1)} %reduce_sum.52), channel_id=1, source_target_pairs={{0,32},{32,0},{64,96},{96,64},{1,33},{33,1},{65,97},{97,65},{2,34}... | collective-permute-start | bytes 221192 | tf_op jit(solution)/shard_map/ppermute | solution.py:94
  214.9 5.2 %collective-permute-start.3 = (f32[24,768]{1,0:T(8,128)S(1)}, f32[24,768]{1,0:T(8,128)S(1)}, u32[]{:S(2)}, u32[]{:S(2)}) collective-permute-start(f32[24,768]{1,0:T(8,128)S(1)} %add.78), channel_id=1, source_target_pairs={{0,64},{32,96},{64,0},{96,32},{1,65},{33,97},{65,1},{97,33},{2,66}... | collective-permute-start | bytes 221192 | tf_op jit(solution)/shard_map/ppermute | solution.py:94
  220.7 41.2 %all-to-all-start.1 = ((bf16[16,128,768]{2,1,0:T(8,128)(2,1)}), bf16[16,128,768]{2,1,0:T(8,128)(2,1)}, u32[]{:S(2)}, u32[]{:S(2)}) async-start(bf16[16,128,768]{2,1,0:T(8,128)(2,1)} %get-tuple-element.28), calls=%async_computation.1 | async-start | bytes 6291456 | tf_op jit(solution)/shard_map/all_to_all | solution.py:99
  264.3 15.6 %copy-start.3 = (bf16[512,768]{1,0:T(8,128)(2,1)S(1)}, bf16[512,768]{1,0:T(8,128)(2,1)}, u32[]{:S(2)}) copy-start(bf16[512,768]{1,0:T(8,128)(2,1)} %copy-done.2) | copy-start | bytes 2359300
  266.4 26.9 %all-to-all-start.2 = ((bf16[128,2,768]{2,1,0:T(2,128)(2,1)}), bf16[128,2,768]{2,1,0:T(2,128)(2,1)S(1)}, u32[]{:S(2)}, u32[]{:S(2)}) async-start(bf16[128,2,768]{2,1,0:T(2,128)(2,1)} %all_to_all.26), calls=%async_computation.2 | async-start | bytes 786432 | tf_op jit(solution)/shard_map/all_to_all | solution.py:104
Sparse Core Ops, SparseCore 0:
  46.3 59.4 all-gather.2
  220.9 71.9 all-gather.4

commit v2 on v0

--- a/solution.py
+++ b/solution.py
@@ -46,8 +46,9 @@
     got_rows = got[:, : 2 * width]
     got_slots = got[:, 2 * width].astype(jnp.int32)
     relaid = jnp.zeros((rows, 2 * width), jnp.bfloat16).at[got_slots].set(got_rows, mode="drop")
-    group_passages = lax.all_gather(relaid[:, :width], MEMBER, axis=0, tiled=True)
-    group_hidden = lax.all_gather(relaid[:, width:], MEMBER, axis=0, tiled=True)
+    group_both = lax.all_gather(relaid, MEMBER, axis=0, tiled=True)
+    group_passages = group_both[:, :width]
+    group_hidden = group_both[:, width:]
     scores = contract(query_emb, group_passages, 1, 1) * factor
     top = jnp.max(scores, axis=1, keepdims=True)
     lse = top[:, 0] + jnp.log(jnp.sum(jnp.exp(scores - top), axis=1))
@@ -76,7 +77,7 @@
         pairs = [(index, index ^ step) for index in range(groups)]
         weight_share = weight_share + lax.ppermute(weight_share, "group", pairs)
         step *= 2
-    grad_weight = lax.all_gather(weight_share, MEMBER, axis=0, tiled=True) / devices
+    grad_weight = lax.all_gather(weight_share / devices, MEMBER, axis=0, tiled=True)
     split = partial.reshape(chips, 2, rows, width)
     kept = jnp.where(core == 0, split[:, 0], split[:, 1])
     given = jnp.where(core == 0, split[:, 1], split[:, 0]).astype(jnp.bfloat16)

time: 280 us -> 269 us (0.961)
  waiting for transfers between devices: 118 us -> 109 us
  other arithmetic: 29 us -> 25.6 us
    all_gather x3 -> x2, waiting for transfers between devices: 63.5 us -> 57.6 us  [the longest x1 57.6 us: body(): group_both = lax.all_gather(relaid, MEMBER, axis=0, tiled=True)]
    dot_general x1, matrix products: 5.62 us -> 9.27 us  [body(): jnp.dot(coef, group_passages, preferred_element_type=jnp.float32)]
  transfers between devices with their start and end apart: 9 -> 8, of which waited for: 7 -> 6; matrix products, arithmetic and copies ran while one was open for 20% -> 8% of each run, Pallas kernels for 0% -> 0%
where the time goes in v2:
time: 269 us; the launch traced here: 268 us
  waiting for transfers between devices  109 us (41%)
  blocking collectives  50.6 us (19%)
  matrix products  33.4 us (12%)
  other arithmetic  25.6 us (10%)
  starting transfers between devices  23.4 us (9%)
  between operations  14.3 us (5%)
  local copies, waits for them, and re-layouts  11.7 us (4%)
    all_gather x1, waiting for transfers between devices, body(): group_both = lax.all_gather(relaid, MEMBER, axis=0, tiled=True)  57.6 us
    all_to_all x1, waiting for transfers between devices, body(): lax.all_to_all(paired.astype(jnp.bfloat16), 'chip', split_axis=0, concat_...  36.8 us
    all_to_all x1, blocking collectives, body(): lax.all_to_all(send_rows, ALL, split_axis=0, concat_axis=0, tiled=True)  28.2 us
    all_to_all x1, blocking collectives, body(): weight_pieces = lax.all_to_all(weight_paired, 'chip', 0, 0, tiled=True)  22.4 us
    dot_general x6, matrix products, contract(): lax.dot_general(left, right, (((left_dim,), (right_dim,)), ((), ())), pre...  20.9 us
    all_to_all x1, starting transfers between devices, body(): lax.all_to_all(back_rows, ALL, split_axis=0, concat_axis=0, tiled=True)  13.9 us
    all_to_all x1, waiting for transfers between devices, body(): lax.all_to_all(back_rows, ALL, split_axis=0, concat_axis=0, tiled=True)  10.5 us
    dot_general x1, matrix products, body(): jnp.dot(coef, group_passages, preferred_element_type=jnp.float32)  9.27 us
  transfers between devices with their start and end apart: 8, of which 6 were waited for; matrix products, arithmetic and copies ran while one was open for 8% of the time, Pallas kernels for 0%

profile of v2, /device:TPU:1, one launch (start us, length us, event | category | flops | bytes accessed | tf_op | source)
XLA Modules:
  0.0 268.1 jit_solution(4397251074235252954)
XLA Ops:
  7.2 0.8 fusion.27
  8.0 0.7 and_select_fusion.1
  8.7 0.2 convert_reduce_fusion
  8.9 1.3 convolution_convert_fusion.3
  10.2 0.1 broadcast_in_dim.11
  10.3 0.1 scatter.22
  10.3 2.1 scatter_custom_fusion
  12.5 0.3 all_to_all.22
  12.8 28.2 %all_to_all.34 = bf16[128,2,1664]{2,1,0:T(2,128)(2,1)} all-to-all(bf16[128,2,1664]{2,1,0:T(2,128)(2,1)S(1)} %all_to_all.22), channel_id=1, replica_groups=mesh['group'=4,'chip'=16,'core'=2] {'group','chip','core'}, dimensions={0} | all-to-all | bytes 1703936 | tf_op jit(solution)/shard_map/all_to_all | solution.py:45
  41.0 2.4 all_to_all.24
  43.4 0.2 fusion.25
  43.6 2.5 scatter_custom_fusion.1
  46.1 1.9 convolution_convert_fusion.1
  48.1 57.6 %all-gather.3.cloned.1.call-done = bf16[4096,1536]{1,0:T(8,128)(2,1)} async-done(((bf16[128,1536]{1,0:T(8,128)(2,1)}), bf16[4096,1536]{1,0:T(8,128)(2,1)}) %all-gather.3.cloned.1.call-update) | async-done | bytes 12582928 | tf_op jit(solution)/shard_map/all_gather | solution.py:49
  105.6 5.8 %multiply_reduce_fusion = (f32[512]{0:T(512)S(1)}, f32[512,4096]{1,0:T(8,128)S(1)}) fusion(bf16[512,768]{1,0:T(8,128)(2,1)S(1)} %convolution_convert_fusion.1, bf16[4096,1536]{1,0:T(8,128)(2,1)} %all-gather.3.cloned.1.call-done), kind=kOutput, calls=%fused_computation.8 | convolution fusion | flops 3225419264 | bytes 15468544 | tf_op jit(solution)/shard_map/dot_general | solution.py:14
  111.5 3.1 %select_reduce_fusion = (f32[512]{0:T(512)S(1)}, f32[512]{0:T(512)S(1)}) fusion(f32[512,4096]{1,0:T(8,128)S(1)} %get-tuple-element.25, s32[512]{0:T(512)S(1)} %copy-done.3, f32[512]{0:T(512)S(1)} %get-tuple-element.24), kind=kLoop, calls=%fused_computation.5 | loop fusion | flops 12581888 | bytes 8396800 | tf_op jit(solution)/shard_map/reduce_sum | solution.py:56
  114.6 0.6 fusion.28
  115.2 3.9 %multiply_convert_fusion = bf16[512,4096]{1,0:T(8,128)(2,1)S(1)} fusion(f32[512,4096]{1,0:T(8,128)S(1)} %get-tuple-element.25, f32[512]{0:T(512)S(1)} %get-tuple-element.21, f32[512]{0:T(512)S(1)} %copy-done.4, s32[512]{0:T(512)S(1)} %copy-done.3), kind=kLoop, calls=%fused_computation.4 | loop fusion | flops 16777216 | bytes 12589056 | tf_op jit(solution)/shard_map/convert_element_type | solution.py:59
  119.1 3.7 %fusion.29 = f32[4096,768]{1,0:T(8,128)S(1)} fusion(bf16[512,4096]{1,0:T(8,128)(2,1)S(1)} %multiply_convert_fusion, bf16[512,768]{1,0:T(8,128)(2,1)S(1)} %convolution_convert_fusion.1), kind=kOutput, calls=%fused_computation.61 | convolution fusion | flops 3221225472 | bytes 17563648 | tf_op jit(solution)/shard_map/dot_general | solution.py:14
  122.7 9.3 %fusion.10 = bf16[512,768]{1,0:T(8,128)(2,1)S(1)} fusion(bf16[512,4096]{1,0:T(8,128)(2,1)S(1)} %multiply_convert_fusion, bf16[4096,1536]{1,0:T(8,128)(2,1)} %all-gather.3.cloned.1.call-done), kind=kOutput, calls=%fused_computation.24 | convolution fusion | flops 3221618688 | bytes 11272192 | tf_op jit(solution)/shard_map/dot_general | solution.py:60
  132.0 7.7 %fusion = f32[768,768]{1,0:T(8,128)S(1)} fusion(f32[4096,768]{1,0:T(8,128)S(1)} %fusion.29, bf16[4096,1536]{1,0:T(8,128)(2,1)} %all-gather.3.cloned.1.call-done), kind=kOutput, calls=%fused_computation.9 | convolution fusion | flops 4831838208 | bytes 21233664 | tf_op jit(solution)/shard_map/dot_general | solution.py:14
  139.8 0.9 bitcast_add_fusion
  140.6 0.1 select_bitcast_fusion
  140.8 0.3 collective-permute-start.1
  141.1 2.2 fusion.9
  143.3 0.3 collective-permute-start
  143.6 0.1 collective-permute-done.1
  143.7 0.2 fusion.14
  143.9 22.4 %all_to_all.35 = f32[16,24,768]{2,1,0:T(8,128)S(1)} all-to-all(f32[16,24,768]{2,1,0:T(8,128)S(1)} %fusion.14), channel_id=1, replica_groups=mesh['group'=4,'chip'=16,'core'=2] {'chip'}, dimensions={0} | all-to-all | bytes 2359296 | tf_op jit(solution)/shard_map/all_to_all | solution.py:73
  166.3 0.1 reduce_sum.52
  166.3 1.4 collective-permute-start.2
  167.7 1.9 collective-permute-done.2
  169.6 3.0 %collective-permute-start.3 = (f32[24,768]{1,0:T(8,128)S(1)}, f32[24,768]{1,0:T(8,128)S(1)}, u32[]{:S(2)}, u32[]{:S(2)}) collective-permute-start(f32[24,768]{1,0:T(8,128)S(1)} %add.61), channel_id=1, source_target_pairs={{0,64},{32,96},{64,0},{96,32},{1,65},{33,97},{65,1},{97,33},{2,66}... | collective-permute-start | bytes 221192 | tf_op jit(solution)/shard_map/ppermute | solution.py:78
  172.6 2.3 collective-permute-done.3
  174.9 0.6 add_multiply_fusion
  175.5 8.5 %fusion.4 = bf16[16,128,768]{2,1,0:T(8,128)(2,1)} fusion(bf16[16,128,768]{2,1,0:T(8,128)(2,1)} %collective-permute-done, f32[16,2,128,768]{3,2,1,0:T(8,128)} %bitcast.64, pred[]{:T(512)S(6)} %eq.40), kind=kLoop, calls=%fused_computation.14 | loop fusion | flops 6291456 | bytes 18874368 | tf_op jit(solution)/shard_map/convert_element_type | solution.py:86
  184.1 4.5 %all-to-all-start.1 = ((bf16[16,128,768]{2,1,0:T(8,128)(2,1)}), bf16[16,128,768]{2,1,0:T(8,128)(2,1)}, u32[]{:S(2)}, u32[]{:S(2)}) async-start(bf16[16,128,768]{2,1,0:T(8,128)(2,1)} %fusion.4), calls=%async_computation.1 | async-start | bytes 6291456 | tf_op jit(solution)/shard_map/all_to_all | solution.py:85
  188.6 36.8 %all-to-all-done.1 = bf16[16,128,768]{2,1,0:T(8,128)(2,1)} async-done(((bf16[16,128,768]{2,1,0:T(8,128)(2,1)}), bf16[16,128,768]{2,1,0:T(8,128)(2,1)}, u32[]{:S(2)}, u32[]{:S(2)}) %all-to-all-start.1) | async-done | bytes 3145760 | tf_op jit(solution)/shard_map/all_to_all | solution.py:85
  225.3 2.3 reduce_sum.51
  227.7 1.2 gather_fusion
  228.9 0.9 all_to_all.26
  229.8 13.9 %all-to-all-start.2 = ((bf16[128,2,768]{2,1,0:T(2,128)(2,1)}), bf16[128,2,768]{2,1,0:T(2,128)(2,1)S(1)}, u32[]{:S(2)}, u32[]{:S(2)}) async-start(bf16[128,2,768]{2,1,0:T(2,128)(2,1)} %all_to_all.26), calls=%async_computation.2 | async-start | bytes 786432 | tf_op jit(solution)/shard_map/all_to_all | solution.py:90
  243.7 1.7 convolution_convert_fusion
  245.4 10.5 %all-to-all-done.2 = bf16[128,2,768]{2,1,0:T(2,128)(2,1)S(1)} async-done(((bf16[128,2,768]{2,1,0:T(2,128)(2,1)}), bf16[128,2,768]{2,1,0:T(2,128)(2,1)S(1)}, u32[]{:S(2)}, u32[]{:S(2)}) %all-to-all-start.2) | async-done | bytes 393248 | tf_op jit(solution)/shard_map/all_to_all | solution.py:90
  255.8 0.1 all_to_all.28
  256.0 0.9 gather_fusion.1
  256.9 1.2 convolution_convert_fusion.2
  258.1 3.2 %copy.47 = f32[768,768]{1,0:T(8,128)} copy(f32[768,768]{1,0:T(8,128)} %all-gather.5.cloned.1.call-done) | data formatting | bytes 4718592
  (22 shorter events, 0.2 us)
Async XLA Ops:
  7.2 1.7 copy-start
  7.2 98.5 %all-gather.3.cloned.1.call-start = ((), (), s32[]{:S(2)}) async-start(), calls=%async_computation.4 | async-start | bytes 12976128 | tf_op jit(solution)/shard_map/all_gather | solution.py:49
  46.1 212.0 %all-gather.5.cloned.1.call-start = ((), (), s32[]{:S(2)}) async-start(), calls=%async_computation.5 | async-start | bytes 2433024 | tf_op jit(solution)/shard_map/all_gather | solution.py:80
  48.0 63.4 %copy-start.3 = (s32[512]{0:T(512)S(1)}, s32[512]{0:T(512)}, u32[]{:S(2)}) copy-start(s32[512]{0:T(512)} %param.14) | copy-start | bytes 6148
  111.5 3.7 %copy-start.4 = (f32[512]{0:T(512)S(1)}, f32[512]{0:T(512)}, u32[]{:S(2)}) copy-start(f32[512]{0:T(512)} %param.15) | copy-start | bytes 6148
  122.7 18.4 %copy-start.1 = (f32[4096,768]{1,0:T(8,128)}, f32[4096,768]{1,0:T(8,128)S(1)}, u32[]{:S(2)}) copy-start(f32[4096,768]{1,0:T(8,128)S(1)} %fusion.29) | copy-start | bytes 37748740
  132.0 7.7 %copy-start.2 = (bf16[512,768]{1,0:T(8,128)(2,1)S(1)}, bf16[512,768]{1,0:T(8,128)(2,1)}, u32[]{:S(2)}) copy-start(bf16[512,768]{1,0:T(8,128)(2,1)} %param.10) | copy-start | bytes 2359300
  140.8 2.9 %collective-permute-start.1 = (f32[16,24,768]{2,1,0:T(8,128)S(1)}, f32[16,24,768]{2,1,0:T(8,128)S(1)}, u32[]{:S(2)}, u32[]{:S(2)}) collective-permute-start(f32[16,24,768]{2,1,0:T(8,128)S(1)} %select_bitcast_fusion), channel_id=1, source_target_pairs={{0,1},{1,0},{2,3},{3,2},{4,5},{5,4},{6,7},{7,6},{8,9},{9,8},{10,11... | collective-permute-start | bytes 3538952 | tf_op jit(solution)/shard_map/ppermute | solution.py:72
  143.3 32.2 %collective-permute-start = (bf16[16,128,768]{2,1,0:T(8,128)(2,1)}, bf16[16,128,768]{2,1,0:T(8,128)(2,1)}, u32[]{:S(2)}, u32[]{:S(2)}) collective-permute-start(bf16[16,128,768]{2,1,0:T(8,128)(2,1)} %fusion.9), channel_id=1, source_target_pairs={{0,1},{1,0},{2,3},{3,2},{4,5},{5,4},{6,7},{7,6},{8,9},{9,8},{10,11... | collective-permute-start | bytes 9437192 | tf_op jit(solution)/shard_map/ppermute | solution.py:84
  166.3 3.3 %collective-permute-start.2 = (f32[24,768]{1,0:T(8,128)S(1)}, f32[24,768]{1,0:T(8,128)S(1)}, u32[]{:S(2)}, u32[]{:S(2)}) collective-permute-start(f32[24,768]{1,0:T(8,128)S(1)} %reduce_sum.52), channel_id=1, source_target_pairs={{0,32},{32,0},{64,96},{96,64},{1,33},{33,1},{65,97},{97,65},{2,34}... | collective-permute-start | bytes 221192 | tf_op jit(solution)/shard_map/ppermute | solution.py:78
  169.6 5.2 %collective-permute-start.3 = (f32[24,768]{1,0:T(8,128)S(1)}, f32[24,768]{1,0:T(8,128)S(1)}, u32[]{:S(2)}, u32[]{:S(2)}) collective-permute-start(f32[24,768]{1,0:T(8,128)S(1)} %add.61), channel_id=1, source_target_pairs={{0,64},{32,96},{64,0},{96,32},{1,65},{33,97},{65,1},{97,33},{2,66}... | collective-permute-start | bytes 221192 | tf_op jit(solution)/shard_map/ppermute | solution.py:78
  184.1 41.3 %all-to-all-start.1 = ((bf16[16,128,768]{2,1,0:T(8,128)(2,1)}), bf16[16,128,768]{2,1,0:T(8,128)(2,1)}, u32[]{:S(2)}, u32[]{:S(2)}) async-start(bf16[16,128,768]{2,1,0:T(8,128)(2,1)} %fusion.4), calls=%async_computation.1 | async-start | bytes 6291456 | tf_op jit(solution)/shard_map/all_to_all | solution.py:85
  229.8 26.1 %all-to-all-start.2 = ((bf16[128,2,768]{2,1,0:T(2,128)(2,1)}), bf16[128,2,768]{2,1,0:T(2,128)(2,1)S(1)}, u32[]{:S(2)}, u32[]{:S(2)}) async-start(bf16[128,2,768]{2,1,0:T(2,128)(2,1)} %all_to_all.26), calls=%async_computation.2 | async-start | bytes 786432 | tf_op jit(solution)/shard_map/all_to_all | solution.py:90
Sparse Core Ops, SparseCore 0:
  46.2 59.4 all-gather.2
  175.6 66.8 all-gather.4

commit v3 on v2

--- a/solution.py
+++ b/solution.py
@@ -46,7 +46,10 @@
     got_rows = got[:, : 2 * width]
     got_slots = got[:, 2 * width].astype(jnp.int32)
     relaid = jnp.zeros((rows, 2 * width), jnp.bfloat16).at[got_slots].set(got_rows, mode="drop")
-    group_both = lax.all_gather(relaid, MEMBER, axis=0, tiled=True)
+    group_both = lax.all_gather(relaid, ("core", "chip"), axis=0, tiled=True)
+    half = group_rows // 2
+    positive_member = positive // rows
+    positive = positive_member % 2 * half + positive_member // 2 * rows + positive % rows
     group_passages = group_both[:, :width]
     group_hidden = group_both[:, width:]
     scores = contract(query_emb, group_passages, 1, 1) * factor
@@ -60,8 +63,18 @@
     query_grad = jnp.dot(coef, group_passages, preferred_element_type=jnp.float32).astype(
         jnp.bfloat16
     )
-    partial = contract(coef, query_emb, 0, 0)
-    local_weight = contract(query_hidden, query_grad, 0, 0) + contract(group_hidden, partial, 0, 0)
+    core = lax.axis_index("core")
+    own_coef = lax.dynamic_slice_in_dim(coef, core * half, half, axis=1)
+    other_coef = lax.dynamic_slice_in_dim(coef, (1 - core) * half, half, axis=1)
+    own_partial = contract(own_coef, query_emb, 0, 0)
+    other_partial = contract(other_coef, query_emb, 0, 0)
+    own_hidden = lax.dynamic_slice_in_dim(group_hidden, core * half, half)
+    other_hidden = lax.dynamic_slice_in_dim(group_hidden, (1 - core) * half, half)
+    local_weight = (
+        contract(query_hidden, query_grad, 0, 0)
+        + contract(own_hidden, own_partial, 0, 0)
+        + contract(other_hidden, other_partial, 0, 0)
+    )
     weight_rows = width // members
     chips = lax.axis_size("chip")
     core = lax.axis_index("core")
@@ -78,9 +91,8 @@
         weight_share = weight_share + lax.ppermute(weight_share, "group", pairs)
         step *= 2
     grad_weight = lax.all_gather(weight_share / devices, MEMBER, axis=0, tiled=True)
-    split = partial.reshape(chips, 2, rows, width)
-    kept = jnp.where(core == 0, split[:, 0], split[:, 1])
-    given = jnp.where(core == 0, split[:, 1], split[:, 0]).astype(jnp.bfloat16)
+    kept = own_partial.reshape(chips, rows, width)
+    given = other_partial.reshape(chips, rows, width).astype(jnp.bfloat16)
     paired = kept + lax.ppermute(given, "core", swap).astype(jnp.float32)
     pieces = lax.all_to_all(
         paired.astype(jnp.bfloat16), "chip", split_axis=0, concat_axis=0, tiled=True

time: 269 us -> 267 us (level)
  matrix products: 33.4 us -> 28.4 us
  waiting for transfers between devices: 109 us -> 114 us
  other arithmetic: 25.6 us -> 21.3 us
  local copies, waits for them, and re-layouts: 11.7 us -> 15.1 us
    dot_general x1, matrix products: 9.27 us -> 3.48 us  [body(): jnp.dot(coef, group_passages, preferred_element_type=jnp.float32)]
    slice x0 -> x1, local copies, waits for them, and re-layouts: none -> 3.33 us  [body(): group_hidden = group_both[:, width:]]
    dot_general x6 -> x8, matrix products: 20.9 us -> 22.9 us  [contract(): lax.dot_general(left, right, (((left_dim,), (right_dim,)), ((), ())), pre...]
  transfers between devices with their start and end apart: 8 -> 8, of which waited for: 6 -> 6; matrix products, arithmetic and copies ran while one was open for 8% -> 6% of each run, Pallas kernels for 0% -> 0%
where the time goes in v3:
time: 267 us
  waiting for transfers between devices  114 us (43%)
  blocking collectives  50.6 us (19%)
  matrix products  28.4 us (11%)
  starting transfers between devices  22.8 us (9%)
  other arithmetic  21.3 us (8%)
  local copies, waits for them, and re-layouts  15.1 us (6%)
  between operations  14.4 us (5%)
    all_gather x1, waiting for transfers between devices, body(): group_both = lax.all_gather(relaid, ('core', 'chip'), axis=0, tiled=True)  58.7 us
    all_to_all x1, waiting for transfers between devices, body(): lax.all_to_all(paired.astype(jnp.bfloat16), 'chip', split_axis=0, concat_...  37.2 us
    all_to_all x1, blocking collectives, body(): lax.all_to_all(send_rows, ALL, split_axis=0, concat_axis=0, tiled=True)  28.2 us
    dot_general x8, matrix products, contract(): lax.dot_general(left, right, (((left_dim,), (right_dim,)), ((), ())), pre...  22.9 us
    all_to_all x1, blocking collectives, body(): weight_pieces = lax.all_to_all(weight_paired, 'chip', 0, 0, tiled=True)  22.4 us
    all_to_all x1, starting transfers between devices, body(): lax.all_to_all(back_rows, ALL, split_axis=0, concat_axis=0, tiled=True)  13.3 us
    all_to_all x1, waiting for transfers between devices, body(): lax.all_to_all(back_rows, ALL, split_axis=0, concat_axis=0, tiled=True)  11.6 us
    convert_element_type x1, other arithmetic, body(): paired.astype(jnp.bfloat16)  6.21 us
  transfers between devices with their start and end apart: 8, of which 6 were waited for; matrix products, arithmetic and copies ran while one was open for 6% of the time, Pallas kernels for 0%

profile of v3, /device:TPU:1, one launch (start us, length us, event | category | flops | bytes accessed | tf_op | source)
XLA Modules:
  0.0 266.6 jit_solution(10821866355711105742)
XLA Ops:
  7.2 0.8 fusion.41
  8.0 0.7 and_select_fusion.1
  8.7 0.2 convert_reduce_fusion
  8.9 1.3 convolution_convert_fusion.3
  10.2 0.1 broadcast_in_dim.11
  10.3 2.1 scatter_custom_fusion
  12.5 0.3 all_to_all.22
  12.8 28.2 %all_to_all.34 = bf16[128,2,1664]{2,1,0:T(2,128)(2,1)} all-to-all(bf16[128,2,1664]{2,1,0:T(2,128)(2,1)S(1)} %all_to_all.22), channel_id=1, replica_groups=mesh['group'=4,'chip'=16,'core'=2] {'group','chip','core'}, dimensions={0} | all-to-all | bytes 1703936 | tf_op jit(solution)/shard_map/all_to_all | solution.py:45
  41.1 2.4 all_to_all.24
  43.5 0.2 fusion.28
  43.7 2.5 scatter_custom_fusion.1
  46.3 0.8 convolution_convert_fusion.1
  47.1 58.7 %all-gather.3.cloned.1.call-done = bf16[4096,1536]{1,0:T(8,128)(2,1)} async-done(((bf16[128,1536]{1,0:T(8,128)(2,1)}), bf16[4096,1536]{1,0:T(8,128)(2,1)}) %all-gather.3.cloned.1.call-update) | async-done | bytes 12582928 | tf_op jit(solution)/shard_map/all_gather | solution.py:49
  105.7 5.8 %multiply_reduce_fusion = (f32[512]{0:T(512)S(1)}, f32[512,4096]{1,0:T(8,128)S(1)}) fusion(bf16[512,768]{1,0:T(8,128)(2,1)S(1)} %convolution_convert_fusion.1, bf16[4096,1536]{1,0:T(8,128)(2,1)} %all-gather.3.cloned.1.call-done), kind=kOutput, calls=%fused_computation.8 | convolution fusion | flops 3225419264 | bytes 15468544 | tf_op jit(solution)/shard_map/dot_general | solution.py:14
  111.5 3.1 %select_reduce_fusion = (f32[512]{0:T(512)S(1)}, f32[512]{0:T(512)S(1)}) fusion(f32[512,4096]{1,0:T(8,128)S(1)} %get-tuple-element.25, s32[512]{0:T(512)S(1)} %fusion.32, f32[512]{0:T(512)S(1)} %get-tuple-element.24), kind=kLoop, calls=%fused_computation.5 | loop fusion | flops 12581888 | bytes 8396800 | tf_op jit(solution)/shard_map/reduce_sum | solution.py:59
  114.6 0.6 fusion.42
  115.2 4.1 %multiply_convert_fusion = bf16[512,4096]{1,0:T(8,128)(2,1)S(1)} fusion(f32[512,4096]{1,0:T(8,128)S(1)} %get-tuple-element.25, f32[512]{0:T(512)S(1)} %get-tuple-element.21, f32[512]{0:T(512)S(1)} %copy-done.5, s32[512]{0:T(512)S(1)} %fusion.32), kind=kLoop, calls=%fused_computation.4 | loop fusion | flops 16777216 | bytes 12589056 | tf_op jit(solution)/shard_map/convert_element_type | solution.py:62
  119.3 1.9 fusion.11
  121.2 3.5 %fusion.9 = bf16[2048,768]{1,0:T(8,128)(2,1)} fusion(bf16[512,768]{1,0:T(8,128)(2,1)S(1)} %convolution_convert_fusion.1, bf16[512,4096]{1,0:T(8,128)(2,1)S(1)} %multiply_convert_fusion, s32[]{:T(128)S(6)} %select_n.82), kind=kOutput, calls=%fused_computation.20 | convolution fusion | flops 1610612736 | bytes 6029316 | tf_op jit(solution)/shard_map/dot_general | solution.py:14
  124.7 3.3 %slice.49 = bf16[4096,768]{1,0:T(8,128)(2,1)S(1)} slice(bf16[4096,1536]{1,0:T(8,128)(2,1)} %all-gather.3.cloned.1.call-done), slice={[0:4096], [768:1536]} | slice | bytes 12582912 | tf_op jit(solution)/shard_map/slice | solution.py:54
  128.1 4.8 %fusion.4 = f32[768,768]{1,0:T(8,128)S(1)} fusion(bf16[2048,768]{1,0:T(8,128)(2,1)} %fusion.9, bf16[4096,768]{1,0:T(8,128)(2,1)S(1)} %slice.49, s32[]{:T(128)S(6)} %select_n.82), kind=kOutput, calls=%fused_computation.14 | convolution fusion | flops 2415919104 | bytes 8650756 | tf_op jit(solution)/shard_map/dot_general | solution.py:14
  132.9 2.8 %fusion.6 = f32[768,768]{1,0:T(8,128)S(1)} fusion(f32[2048,768]{1,0:T(8,128)S(1)} %fusion.11, bf16[4096,768]{1,0:T(8,128)(2,1)S(1)} %slice.49, s32[]{:T(128)S(6)} %select_n.81), kind=kOutput, calls=%fused_computation.16 | convolution fusion | flops 2415919104 | bytes 11796484 | tf_op jit(solution)/shard_map/dot_general | solution.py:14
  135.8 3.5 %fusion.13 = bf16[512,768]{1,0:T(8,128)(2,1)S(1)} fusion(bf16[512,4096]{1,0:T(8,128)(2,1)S(1)} %multiply_convert_fusion, bf16[4096,1536]{1,0:T(8,128)(2,1)S(1)} %bitcast.45), kind=kOutput, calls=%fused_computation.26 | convolution fusion | flops 3221618688 | bytes 11272192 | tf_op jit(solution)/shard_map/dot_general | solution.py:63
  139.3 1.2 fusion.8
  140.5 0.1 select_bitcast_fusion
  140.6 0.3 collective-permute-start.1
  141.0 0.2 collective-permute-start
  141.2 2.3 collective-permute-done.1
  143.5 0.2 fusion.17
  143.7 22.4 %all_to_all.35 = f32[16,24,768]{2,1,0:T(8,128)S(1)} all-to-all(f32[16,24,768]{2,1,0:T(8,128)S(1)} %fusion.17), channel_id=1, replica_groups=mesh['group'=4,'chip'=16,'core'=2] {'chip'}, dimensions={0} | all-to-all | bytes 2359296 | tf_op jit(solution)/shard_map/all_to_all | solution.py:86
  166.2 1.4 collective-permute-start.2
  167.6 1.9 collective-permute-done.2
  169.5 2.9 %collective-permute-start.3 = (f32[24,768]{1,0:T(8,128)S(1)}, f32[24,768]{1,0:T(8,128)S(1)}, u32[]{:S(2)}, u32[]{:S(2)}) collective-permute-start(f32[24,768]{1,0:T(8,128)S(1)} %add.97), channel_id=1, source_target_pairs={{0,64},{32,96},{64,0},{96,32},{1,65},{33,97},{65,1},{97,33},{2,66}... | collective-permute-start | bytes 221192 | tf_op jit(solution)/shard_map/ppermute | solution.py:91
  172.4 2.3 collective-permute-done.3
  174.7 0.6 add_multiply_fusion
  175.4 6.2 %add_convert_fusion = bf16[16,128,768]{2,1,0:T(8,128)(2,1)} fusion(f32[16,128,768]{2,1,0:T(8,128)} %bitcast.41, bf16[16,128,768]{2,1,0:T(8,128)(2,1)} %collective-permute-done), kind=kLoop, calls=%fused_computation.9 | loop fusion | flops 4718592 | bytes 12582912 | tf_op jit(solution)/shard_map/convert_element_type | solution.py:98
  181.6 4.5 %all-to-all-start.1 = ((bf16[16,128,768]{2,1,0:T(8,128)(2,1)}), bf16[16,128,768]{2,1,0:T(8,128)(2,1)}, u32[]{:S(2)}, u32[]{:S(2)}) async-start(bf16[16,128,768]{2,1,0:T(8,128)(2,1)} %add_convert_fusion), calls=%async_computation.1 | async-start | bytes 6291456 | tf_op jit(solution)/shard_map/all_to_all | solution.py:97
  186.1 37.2 %all-to-all-done.1 = bf16[16,128,768]{2,1,0:T(8,128)(2,1)} async-done(((bf16[16,128,768]{2,1,0:T(8,128)(2,1)}), bf16[16,128,768]{2,1,0:T(8,128)(2,1)}, u32[]{:S(2)}, u32[]{:S(2)}) %all-to-all-start.1) | async-done | bytes 3145760 | tf_op jit(solution)/shard_map/all_to_all | solution.py:97
  223.3 2.3 reduce_sum.51
  225.7 1.2 gather_fusion
  226.9 0.9 all_to_all.26
  227.8 13.3 %all-to-all-start.2 = ((bf16[128,2,768]{2,1,0:T(2,128)(2,1)}), bf16[128,2,768]{2,1,0:T(2,128)(2,1)S(1)}, u32[]{:S(2)}, u32[]{:S(2)}) async-start(bf16[128,2,768]{2,1,0:T(2,128)(2,1)} %all_to_all.26), calls=%async_computation.2 | async-start | bytes 786432 | tf_op jit(solution)/shard_map/all_to_all | solution.py:102
  241.1 1.7 convolution_convert_fusion
  242.8 11.6 %all-to-all-done.2 = bf16[128,2,768]{2,1,0:T(2,128)(2,1)S(1)} async-done(((bf16[128,2,768]{2,1,0:T(2,128)(2,1)}), bf16[128,2,768]{2,1,0:T(2,128)(2,1)S(1)}, u32[]{:S(2)}, u32[]{:S(2)}) %all-to-all-start.2) | async-done | bytes 393248 | tf_op jit(solution)/shard_map/all_to_all | solution.py:102
  254.3 0.1 all_to_all.28
  254.5 0.9 gather_fusion.1
  255.4 1.2 convolution_convert_fusion.2
  256.6 3.2 %copy.30 = f32[768,768]{1,0:T(8,128)} copy(f32[768,768]{1,0:T(8,128)} %all-gather.5.cloned.1.call-done) | data formatting | bytes 4718592
  (36 shorter events, 0.4 us)
Async XLA Ops:
  7.2 1.7 copy-start
  7.2 98.5 %all-gather.3.cloned.1.call-start = ((), (), s32[]{:S(2)}) async-start(), calls=%async_computation.4 | async-start | bytes 12976128 | tf_op jit(solution)/shard_map/all_gather | solution.py:49
  12.5 33.8 %copy-start.6 = (s32[512]{0:T(512)S(1)}, s32[512]{0:T(512)}, u32[]{:S(2)}) copy-start(s32[512]{0:T(512)} %param.14) | copy-start | bytes 6148
  41.1 5.2 %copy-start.2 = (bf16[512,768]{1,0:T(8,128)(2,1)S(1)}, bf16[512,768]{1,0:T(8,128)(2,1)}, u32[]{:S(2)}) copy-start(bf16[512,768]{1,0:T(8,128)(2,1)} %param.10) | copy-start | bytes 2359300
  46.2 210.4 %all-gather.5.cloned.1.call-start = ((), (), s32[]{:S(2)}) async-start(), calls=%async_computation.5 | async-start | bytes 2433024 | tf_op jit(solution)/shard_map/all_gather | solution.py:93
  111.5 3.7 %copy-start.5 = (f32[512]{0:T(512)S(1)}, f32[512]{0:T(512)}, u32[]{:S(2)}) copy-start(f32[512]{0:T(512)} %param.15) | copy-start | bytes 6148
  121.2 11.7 %copy-start.1 = (f32[2048,768]{1,0:T(8,128)}, f32[2048,768]{1,0:T(8,128)S(1)}, u32[]{:S(2)}) copy-start(f32[2048,768]{1,0:T(8,128)S(1)} %fusion.11) | copy-start | bytes 18874372
  128.1 7.7 %slice-start = ((s8[12582912]{0:T(1024)(128)(4,1)}), s8[4194304]{0:T(1024)(128)(4,1)S(1)}, s32[]{:S(2)}) async-start(s8[12582912]{0:T(1024)(128)(4,1)} %bitcast.44), calls=%async_computation.6 | async-start | bytes 8388608
  128.1 7.7 %slice-start.1 = ((s8[12582912]{0:T(1024)(128)(4,1)}), s8[4194304]{0:T(1024)(128)(4,1)S(1)}, s32[]{:S(2)}) async-start(s8[12582912]{0:T(1024)(128)(4,1)} %bitcast.44), calls=%async_computation.7 | async-start | bytes 8388608
  132.9 2.9 %slice-start.2 = ((s8[12582912]{0:T(1024)(128)(4,1)}), s8[4194304]{0:T(1024)(128)(4,1)S(1)}, s32[]{:S(2)}) async-start(s8[12582912]{0:T(1024)(128)(4,1)} %bitcast.44), calls=%async_computation.8 | async-start | bytes 8388608
  139.3 1.2 copy-start.3
  140.6 2.9 %collective-permute-start.1 = (f32[16,24,768]{2,1,0:T(8,128)S(1)}, f32[16,24,768]{2,1,0:T(8,128)S(1)}, u32[]{:S(2)}, u32[]{:S(2)}) collective-permute-start(f32[16,24,768]{2,1,0:T(8,128)S(1)} %select_bitcast_fusion), channel_id=1, source_target_pairs={{0,1},{1,0},{2,3},{3,2},{4,5},{5,4},{6,7},{7,6},{8,9},{9,8},{10,11... | collective-permute-start | bytes 3538952 | tf_op jit(solution)/shard_map/ppermute | solution.py:85
  141.0 34.4 %collective-permute-start = (bf16[16,128,768]{2,1,0:T(8,128)(2,1)}, bf16[16,128,768]{2,1,0:T(8,128)(2,1)}, u32[]{:S(2)}, u32[]{:S(2)}) collective-permute-start(bf16[16,128,768]{2,1,0:T(8,128)(2,1)} %bitcast.1), channel_id=1, source_target_pairs={{0,1},{1,0},{2,3},{3,2},{4,5},{5,4},{6,7},{7,6},{8,9},{9,8},{10,11... | collective-permute-start | bytes 9437192 | tf_op jit(solution)/shard_map/ppermute | solution.py:96
  166.2 3.3 %collective-permute-start.2 = (f32[24,768]{1,0:T(8,128)S(1)}, f32[24,768]{1,0:T(8,128)S(1)}, u32[]{:S(2)}, u32[]{:S(2)}) collective-permute-start(f32[24,768]{1,0:T(8,128)S(1)} %reduce_sum.52), channel_id=1, source_target_pairs={{0,32},{32,0},{64,96},{96,64},{1,33},{33,1},{65,97},{97,65},{2,34}... | collective-permute-start | bytes 221192 | tf_op jit(solution)/shard_map/ppermute | solution.py:91
  169.5 5.2 %collective-permute-start.3 = (f32[24,768]{1,0:T(8,128)S(1)}, f32[24,768]{1,0:T(8,128)S(1)}, u32[]{:S(2)}, u32[]{:S(2)}) collective-permute-start(f32[24,768]{1,0:T(8,128)S(1)} %add.97), channel_id=1, source_target_pairs={{0,64},{32,96},{64,0},{96,32},{1,65},{33,97},{65,1},{97,33},{2,66}... | collective-permute-start | bytes 221192 | tf_op jit(solution)/shard_map/ppermute | solution.py:91
  181.6 41.7 %all-to-all-start.1 = ((bf16[16,128,768]{2,1,0:T(8,128)(2,1)}), bf16[16,128,768]{2,1,0:T(8,128)(2,1)}, u32[]{:S(2)}, u32[]{:S(2)}) async-start(bf16[16,128,768]{2,1,0:T(8,128)(2,1)} %add_convert_fusion), calls=%async_computation.1 | async-start | bytes 6291456 | tf_op jit(solution)/shard_map/all_to_all | solution.py:97
  225.7 15.4 %copy-start.4 = (bf16[512,768]{1,0:T(8,128)(2,1)S(1)}, bf16[512,768]{1,0:T(8,128)(2,1)}, u32[]{:S(2)}) copy-start(bf16[512,768]{1,0:T(8,128)(2,1)} %copy-done.3) | copy-start | bytes 2359300
  227.8 26.6 %all-to-all-start.2 = ((bf16[128,2,768]{2,1,0:T(2,128)(2,1)}), bf16[128,2,768]{2,1,0:T(2,128)(2,1)S(1)}, u32[]{:S(2)}, u32[]{:S(2)}) async-start(bf16[128,2,768]{2,1,0:T(2,128)(2,1)} %all_to_all.26), calls=%async_computation.2 | async-start | bytes 786432 | tf_op jit(solution)/shard_map/all_to_all | solution.py:102
Sparse Core Ops, SparseCore 0:
  46.3 59.3 all-gather.2
  175.5 76.1 all-gather.4

commit v4 on v2

--- a/solution.py
+++ b/solution.py
@@ -6,7 +6,6 @@
 from jax.sharding import PartitionSpec as P
 
 
-MEMBER = ("chip", "core")
 ALL = ("group", "chip", "core")
 
 
@@ -46,7 +45,10 @@
     got_rows = got[:, : 2 * width]
     got_slots = got[:, 2 * width].astype(jnp.int32)
     relaid = jnp.zeros((rows, 2 * width), jnp.bfloat16).at[got_slots].set(got_rows, mode="drop")
-    group_both = lax.all_gather(relaid, MEMBER, axis=0, tiled=True)
+    group_both = lax.all_gather(relaid, ("core", "chip"), axis=0, tiled=True)
+    half = group_rows // 2
+    positive_member = positive // rows
+    positive = positive_member % 2 * half + positive_member // 2 * rows + positive % rows
     group_passages = group_both[:, :width]
     group_hidden = group_both[:, width:]
     scores = contract(query_emb, group_passages, 1, 1) * factor
@@ -62,25 +64,21 @@
     )
     partial = contract(coef, query_emb, 0, 0)
     local_weight = contract(query_hidden, query_grad, 0, 0) + contract(group_hidden, partial, 0, 0)
-    weight_rows = width // members
     chips = lax.axis_size("chip")
     core = lax.axis_index("core")
     swap = [(0, 1), (1, 0)]
-    weight_split = local_weight.reshape(chips, 2, weight_rows, width)
-    weight_kept = jnp.where(core == 0, weight_split[:, 0], weight_split[:, 1])
-    weight_given = jnp.where(core == 0, weight_split[:, 1], weight_split[:, 0])
+    weight_split = local_weight.reshape(2, groups * chips, width // devices, width)
+    weight_kept = jnp.where(core == 0, weight_split[0], weight_split[1])
+    weight_given = jnp.where(core == 0, weight_split[1], weight_split[0])
     weight_paired = weight_kept + lax.ppermute(weight_given, "core", swap)
-    weight_pieces = lax.all_to_all(weight_paired, "chip", 0, 0, tiled=True)
+    weight_pieces = lax.all_to_all(weight_paired, ("group", "chip"), 0, 0, tiled=True)
     weight_share = jnp.sum(weight_pieces, axis=0)
-    step = 1
-    while step < groups:
-        pairs = [(index, index ^ step) for index in range(groups)]
-        weight_share = weight_share + lax.ppermute(weight_share, "group", pairs)
-        step *= 2
-    grad_weight = lax.all_gather(weight_share / devices, MEMBER, axis=0, tiled=True)
-    split = partial.reshape(chips, 2, rows, width)
-    kept = jnp.where(core == 0, split[:, 0], split[:, 1])
-    given = jnp.where(core == 0, split[:, 1], split[:, 0]).astype(jnp.bfloat16)
+    grad_weight = lax.all_gather(
+        weight_share / devices, ("core", "group", "chip"), axis=0, tiled=True
+    )
+    kept = lax.dynamic_slice_in_dim(partial, core * half, half).reshape(chips, rows, width)
+    given = lax.dynamic_slice_in_dim(partial, (1 - core) * half, half)
+    given = given.reshape(chips, rows, width).astype(jnp.bfloat16)
     paired = kept + lax.ppermute(given, "core", swap).astype(jnp.float32)
     pieces = lax.all_to_all(
         paired.astype(jnp.bfloat16), "chip", split_axis=0, concat_axis=0, tiled=True

time: 269 us -> 279 us (1.037)
  local copies, waits for them, and re-layouts: 11.7 us -> 25.5 us
  blocking collectives: 50.6 us -> 59.3 us
  starting transfers between devices: 23.4 us -> 15.6 us
  matrix products: 33.4 us -> 27.4 us
  waiting for transfers between devices: 109 us -> 112 us
    all_to_all x1, blocking collectives: 22.4 us -> 31.1 us  [body(): lax.all_to_all(weight_paired, ('group', 'chip'), 0, 0, tiled=True)]
    all_gather x2, waiting for transfers between devices: 57.6 us -> 63.5 us  [the longest x1 57.4 us: body(): group_both = lax.all_gather(relaid, ('core', 'chip'), axis=0, tiled=True)]
    dot_general x1, matrix products: 9.27 us -> 3.46 us  [body(): jnp.dot(coef, group_passages, preferred_element_type=jnp.float32)]
    convert_element_type x0 -> x1, local copies, waits for them, and re-layouts: none -> 4.77 us  [body(): given = given.reshape(chips, rows, width).astype(jnp.bfloat16)]
    ppermute x2 -> x0, starting transfers between devices: 4.32 us -> none  [body(): weight_share = weight_share + lax.ppermute(weight_share, 'group', pairs)]
    ppermute x2 -> x0, waiting for transfers between devices: 4.19 us -> none  [body(): weight_share = weight_share + lax.ppermute(weight_share, 'group', pairs)]
    convert_element_type x1, other arithmetic: 8.52 us -> 4.36 us  [body(): paired.astype(jnp.bfloat16)]
    select_n x0 -> x3, local copies, waits for them, and re-layouts: none -> 4.16 us  [the longest x2 2.77 us: body(): weight_given = jnp.where(core == 0, weight_split[1], weight_split[0])]
  transfers between devices with their start and end apart: 8 -> 6, of which waited for: 6 -> 4; matrix products, arithmetic and copies ran while one was open for 8% -> 10% of each run, Pallas kernels for 0% -> 0%
where the time goes in v4:
time: 279 us; the launch traced here: 278 us
  waiting for transfers between devices  112 us (40%)
  blocking collectives  59.3 us (21%)
  matrix products  27.4 us (10%)
  local copies, waits for them, and re-layouts  25.5 us (9%)
  other arithmetic  24 us (9%)
  starting transfers between devices  15.6 us (6%)
  between operations  14.4 us (5%)
    all_gather x1, waiting for transfers between devices, body(): group_both = lax.all_gather(relaid, ('core', 'chip'), axis=0, tiled=True)  57.4 us
    all_to_all x1, waiting for transfers between devices, body(): lax.all_to_all(paired.astype(jnp.bfloat16), 'chip', split_axis=0, concat_...  37.4 us
    all_to_all x1, blocking collectives, body(): lax.all_to_all(weight_paired, ('group', 'chip'), 0, 0, tiled=True)  31.1 us
    all_to_all x1, blocking collectives, body(): lax.all_to_all(send_rows, ALL, split_axis=0, concat_axis=0, tiled=True)  28.2 us
    dot_general x6, matrix products, contract(): lax.dot_general(left, right, (((left_dim,), (right_dim,)), ((), ())), pre...  20.7 us
    all_to_all x1, waiting for transfers between devices, body(): lax.all_to_all(back_rows, ALL, split_axis=0, concat_axis=0, tiled=True)  10.9 us
    all_to_all x1, starting transfers between devices, body(): lax.all_to_all(back_rows, ALL, split_axis=0, concat_axis=0, tiled=True)  10.3 us
    all_gather x1, waiting for transfers between devices, body(): lax.all_gather(weight_share / devices, ('core', 'group', 'chip'), axis=0,...  6.13 us
  transfers between devices with their start and end apart: 6, of which 4 were waited for; matrix products, arithmetic and copies ran while one was open for 10% of the time, Pallas kernels for 0%

profile of v4, /device:TPU:1, one launch (start us, length us, event | category | flops | bytes accessed | tf_op | source)
XLA Modules:
  0.0 277.9 jit_solution(7106320283711485450)
XLA Ops:
  7.2 0.8 fusion.28
  8.0 0.7 and_select_fusion.1
  8.7 0.2 convert_reduce_fusion
  8.9 1.3 convolution_convert_fusion.3
  10.3 2.1 scatter_custom_fusion
  12.5 0.3 all_to_all.22
  12.8 28.2 %all_to_all.34 = bf16[128,2,1664]{2,1,0:T(2,128)(2,1)} all-to-all(bf16[128,2,1664]{2,1,0:T(2,128)(2,1)S(1)} %all_to_all.22), channel_id=1, replica_groups=mesh['group'=4,'chip'=16,'core'=2] {'group','chip','core'}, dimensions={0} | all-to-all | bytes 1703936 | tf_op jit(solution)/shard_map/all_to_all | solution.py:44
  41.1 2.4 all_to_all.24
  43.4 0.2 fusion.19
  43.6 2.5 scatter_custom_fusion.1
  46.1 0.2 all-gather.6.cloned.1.call-start
  46.4 1.9 convolution_convert_fusion.1
  48.3 57.4 %all-gather.4.cloned.1.call-done = bf16[4096,1536]{1,0:T(8,128)(2,1)} async-done(((bf16[128,1536]{1,0:T(8,128)(2,1)}), bf16[4096,1536]{1,0:T(8,128)(2,1)}) %all-gather.4.cloned.1.call-update) | async-done | bytes 12582928 | tf_op jit(solution)/shard_map/all_gather | solution.py:48
  105.6 5.8 %multiply_reduce_fusion = (f32[512]{0:T(512)S(1)}, f32[512,4096]{1,0:T(8,128)S(1)}) fusion(bf16[512,768]{1,0:T(8,128)(2,1)S(1)} %convolution_convert_fusion.1, bf16[4096,1536]{1,0:T(8,128)(2,1)} %all-gather.4.cloned.1.call-done), kind=kOutput, calls=%fused_computation.8 | convolution fusion | flops 3225419264 | bytes 15468544 | tf_op jit(solution)/shard_map/dot_general | solution.py:13
  111.5 3.1 %select_reduce_fusion = (f32[512]{0:T(512)S(1)}, f32[512]{0:T(512)S(1)}) fusion(f32[512,4096]{1,0:T(8,128)S(1)} %get-tuple-element.27, s32[512]{0:T(512)S(1)} %fusion.23, f32[512]{0:T(512)S(1)} %get-tuple-element.26), kind=kLoop, calls=%fused_computation.5 | loop fusion | flops 12581888 | bytes 8396800 | tf_op jit(solution)/shard_map/reduce_sum | solution.py:58
  114.6 0.6 fusion.29
  115.2 3.9 %multiply_convert_fusion = bf16[512,4096]{1,0:T(8,128)(2,1)S(1)} fusion(f32[512,4096]{1,0:T(8,128)S(1)} %get-tuple-element.27, f32[512]{0:T(512)S(1)} %get-tuple-element.21, f32[512]{0:T(512)S(1)} %copy-done.3, s32[512]{0:T(512)S(1)} %fusion.23), kind=kLoop, calls=%fused_computation.4 | loop fusion | flops 16777216 | bytes 12589056 | tf_op jit(solution)/shard_map/convert_element_type | solution.py:61
  119.1 3.6 %fusion.30 = f32[4096,768]{1,0:T(8,128)S(1)} fusion(bf16[512,4096]{1,0:T(8,128)(2,1)S(1)} %multiply_convert_fusion, bf16[512,768]{1,0:T(8,128)(2,1)S(1)} %convolution_convert_fusion.1), kind=kOutput, calls=%fused_computation.76 | convolution fusion | flops 3221225472 | bytes 17563648 | tf_op jit(solution)/shard_map/dot_general | solution.py:13
  122.7 3.5 %fusion.6 = bf16[512,768]{1,0:T(8,128)(2,1)S(1)} fusion(bf16[512,4096]{1,0:T(8,128)(2,1)S(1)} %multiply_convert_fusion, bf16[4096,1536]{1,0:T(8,128)(2,1)S(1)} %bitcast.25), kind=kOutput, calls=%fused_computation.21 | convolution fusion | flops 3221618688 | bytes 11272192 | tf_op jit(solution)/shard_map/dot_general | solution.py:62
  126.2 1.1 copy-done.1
  127.3 7.5 %fusion = f32[768,768]{1,0:T(8,128)S(1)} fusion(f32[4096,768]{1,0:T(8,128)S(1)} %fusion.30, bf16[4096,1536]{1,0:T(8,128)(2,1)} %all-gather.4.cloned.1.call-done), kind=kOutput, calls=%fused_computation.9 | convolution fusion | flops 4831838208 | bytes 21233664 | tf_op jit(solution)/shard_map/dot_general | solution.py:13
  134.8 0.9 bitcast_add_fusion
  135.7 1.6 slice_select_fusion
  137.3 1.4 select_n.86
  138.8 1.4 copy.13
  140.1 0.3 collective-permute-start.1
  140.4 4.8 %dynamic-slice_convert_fusion = bf16[2048,768]{1,0:T(8,128)(2,1)} fusion(f32[4096,768]{1,0:T(8,128)} %copy-done.1, s32[]{:T(128)S(6)} %select_n.80), kind=kLoop, calls=%fused_computation.12 | loop fusion | bytes 6291460 | tf_op jit(solution)/shard_map/convert_element_type | solution.py:81
  145.2 0.2 collective-permute-start
  145.4 1.4 select_n.84
  146.8 2.0 copy_add_fusion
  148.8 31.1 %all_to_all.35 = f32[64,6,768]{2,1,0:T(8,128)S(1)} all-to-all(f32[64,6,768]{2,1,0:T(8,128)S(1)} %copy_add_fusion), channel_id=1, replica_groups=mesh['group'=4,'chip'=16,'core'=2] {'group','chip'}, dimensions={0} | all-to-all | bytes 2359296 | tf_op jit(solution)/shard_map/all_to_all | solution.py:74
  179.9 0.7 reduce_sum.52
  180.6 1.3 multiply_bitcast_fusion
  182.0 3.2 %constant_dynamic-slice_fusion = f32[2048,768]{1,0:T(8,128)S(1)} fusion(f32[4096,768]{1,0:T(8,128)} %copy-done.1, s32[]{:T(128)S(6)} %select_n.79), kind=kLoop, calls=%fused_computation.73 | loop fusion | bytes 12582916 | tf_op jit(solution)/shard_map/dynamic_slice | solution.py:79
  185.2 4.4 %add_convert_fusion = bf16[16,128,768]{2,1,0:T(8,128)(2,1)} fusion(f32[16,128,768]{2,1,0:T(8,128)S(1)} %bitcast.23, bf16[16,128,768]{2,1,0:T(8,128)(2,1)} %collective-permute-done), kind=kLoop, calls=%fused_computation.11 | loop fusion | flops 4718592 | bytes 12582912 | tf_op jit(solution)/shard_map/convert_element_type | solution.py:84
  189.6 4.5 %all-to-all-start.1 = ((bf16[16,128,768]{2,1,0:T(8,128)(2,1)}), bf16[16,128,768]{2,1,0:T(8,128)(2,1)}, u32[]{:S(2)}, u32[]{:S(2)}) async-start(bf16[16,128,768]{2,1,0:T(8,128)(2,1)} %add_convert_fusion), calls=%async_computation.1 | async-start | bytes 6291456 | tf_op jit(solution)/shard_map/all_to_all | solution.py:83
  194.1 37.4 %all-to-all-done.1 = bf16[16,128,768]{2,1,0:T(8,128)(2,1)} async-done(((bf16[16,128,768]{2,1,0:T(8,128)(2,1)}), bf16[16,128,768]{2,1,0:T(8,128)(2,1)}, u32[]{:S(2)}, u32[]{:S(2)}) %all-to-all-start.1) | async-done | bytes 3145760 | tf_op jit(solution)/shard_map/all_to_all | solution.py:83
  231.5 2.3 reduce_sum.51
  233.8 1.2 gather_fusion
  235.0 0.9 all_to_all.26
  235.9 10.3 %all-to-all-start.2 = ((bf16[128,2,768]{2,1,0:T(2,128)(2,1)}), bf16[128,2,768]{2,1,0:T(2,128)(2,1)S(1)}, u32[]{:S(2)}, u32[]{:S(2)}) async-start(bf16[128,2,768]{2,1,0:T(2,128)(2,1)} %all_to_all.26), calls=%async_computation.2 | async-start | bytes 786432 | tf_op jit(solution)/shard_map/all_to_all | solution.py:88
  246.2 1.7 convolution_convert_fusion
  247.9 10.9 %all-to-all-done.2 = bf16[128,2,768]{2,1,0:T(2,128)(2,1)S(1)} async-done(((bf16[128,2,768]{2,1,0:T(2,128)(2,1)}), bf16[128,2,768]{2,1,0:T(2,128)(2,1)S(1)}, u32[]{:S(2)}, u32[]{:S(2)}) %all-to-all-start.2) | async-done | bytes 393248 | tf_op jit(solution)/shard_map/all_to_all | solution.py:88
  258.8 0.1 all_to_all.28
  258.9 0.9 gather_fusion.1
  259.8 1.2 convolution_convert_fusion.2
  261.0 6.1 %all-gather.6.cloned.1.call-done = f32[128,6,768]{2,1,0:T(8,128)} async-done(((f32[1,6,768]{2,1,0:T(8,128)}), f32[128,6,768]{2,1,0:T(8,128)}) %all-gather.6.cloned.1.call-update) | async-done | bytes 2359312 | tf_op jit(solution)/shard_map/all_gather | solution.py:76
  267.2 3.9 %reshape.98 = f32[768,768]{1,0:T(8,128)} reshape(f32[128,6,768]{2,1,0:T(8,128)} %all-gather.6.cloned.1.call-done) | data formatting | bytes 4718592
  (29 shorter events, 0.3 us)
Async XLA Ops:
  7.2 1.7 copy-start
  7.2 98.5 %all-gather.4.cloned.1.call-start = ((), (), s32[]{:S(2)}) async-start(), calls=%async_computation.4 | async-start | bytes 12976128 | tf_op jit(solution)/shard_map/all_gather | solution.py:48
  10.3 36.0 %copy-start.4 = (s32[512]{0:T(512)S(1)}, s32[512]{0:T(512)}, u32[]{:S(2)}) copy-start(s32[512]{0:T(512)} %param.14) | copy-start | bytes 6148
  46.1 221.1 %all-gather.6.cloned.1.call-start = ((), (), s32[]{:S(2)}) async-start(), calls=%async_computation.5 | async-start | bytes 3170304 | tf_op jit(solution)/shard_map/all_gather | solution.py:76
  111.4 3.7 %copy-start.3 = (f32[512]{0:T(512)S(1)}, f32[512]{0:T(512)}, u32[]{:S(2)}) copy-start(f32[512]{0:T(512)} %param.15) | copy-start | bytes 6148
  115.1 7.5 %slice-start = ((s8[12582912]{0:T(1024)(128)(4,1)}), s8[4194304]{0:T(1024)(128)(4,1)S(1)}, s32[]{:S(2)}) async-start(s8[12582912]{0:T(1024)(128)(4,1)} %bitcast.24), calls=%async_computation.6 | async-start | bytes 8388608
  115.2 7.5 %slice-start.1 = ((s8[12582912]{0:T(1024)(128)(4,1)}), s8[4194304]{0:T(1024)(128)(4,1)S(1)}, s32[]{:S(2)}) async-start(s8[12582912]{0:T(1024)(128)(4,1)} %bitcast.24), calls=%async_computation.7 | async-start | bytes 8388608
  119.1 3.6 %slice-start.2 = ((s8[12582912]{0:T(1024)(128)(4,1)}), s8[4194304]{0:T(1024)(128)(4,1)S(1)}, s32[]{:S(2)}) async-start(s8[12582912]{0:T(1024)(128)(4,1)} %bitcast.24), calls=%async_computation.8 | async-start | bytes 8388608
  122.7 4.6 %copy-start.1 = (f32[4096,768]{1,0:T(8,128)}, f32[4096,768]{1,0:T(8,128)S(1)}, u32[]{:S(2)}) copy-start(f32[4096,768]{1,0:T(8,128)S(1)} %fusion.30) | copy-start | bytes 37748740
  127.3 7.6 %copy-start.2 = (bf16[512,768]{1,0:T(8,128)(2,1)S(1)}, bf16[512,768]{1,0:T(8,128)(2,1)}, u32[]{:S(2)}) copy-start(bf16[512,768]{1,0:T(8,128)(2,1)} %param.10) | copy-start | bytes 2359300
  140.1 6.7 %collective-permute-start.1 = (f32[64,6,768]{2,0,1:T(8,128)}, f32[64,6,768]{2,0,1:T(8,128)}, u32[]{:S(2)}, u32[]{:S(2)}) collective-permute-start(f32[64,6,768]{2,0,1:T(8,128)} %copy.13), channel_id=1, source_target_pairs={{0,1},{1,0},{2,3},{3,2},{4,5},{5,4},{6,7},{7,6},{8,9},{9,8},{10,11... | collective-permute-start | bytes 3538952 | tf_op jit(solution)/shard_map/ppermute | solution.py:73
  145.2 40.1 %collective-permute-start = (bf16[16,128,768]{2,1,0:T(8,128)(2,1)}, bf16[16,128,768]{2,1,0:T(8,128)(2,1)}, u32[]{:S(2)}, u32[]{:S(2)}) collective-permute-start(bf16[16,128,768]{2,1,0:T(8,128)(2,1)} %bitcast.1), channel_id=1, source_target_pairs={{0,1},{1,0},{2,3},{3,2},{4,5},{5,4},{6,7},{7,6},{8,9},{9,8},{10,11... | collective-permute-start | bytes 9437192 | tf_op jit(solution)/shard_map/ppermute | solution.py:82
  189.6 41.9 %all-to-all-start.1 = ((bf16[16,128,768]{2,1,0:T(8,128)(2,1)}), bf16[16,128,768]{2,1,0:T(8,128)(2,1)}, u32[]{:S(2)}, u32[]{:S(2)}) async-start(bf16[16,128,768]{2,1,0:T(8,128)(2,1)} %add_convert_fusion), calls=%async_computation.1 | async-start | bytes 6291456 | tf_op jit(solution)/shard_map/all_to_all | solution.py:83
  235.9 22.9 %all-to-all-start.2 = ((bf16[128,2,768]{2,1,0:T(2,128)(2,1)}), bf16[128,2,768]{2,1,0:T(2,128)(2,1)S(1)}, u32[]{:S(2)}, u32[]{:S(2)}) async-start(bf16[128,2,768]{2,1,0:T(2,128)(2,1)} %all_to_all.26), calls=%async_computation.2 | async-start | bytes 786432 | tf_op jit(solution)/shard_map/all_to_all | solution.py:88
Sparse Core Ops, SparseCore 0:
  46.2 59.3 all-gather.3
  182.1 84.9 all-gather.5

commit v5 on v2

--- a/solution.py
+++ b/solution.py
@@ -46,7 +46,10 @@
     got_rows = got[:, : 2 * width]
     got_slots = got[:, 2 * width].astype(jnp.int32)
     relaid = jnp.zeros((rows, 2 * width), jnp.bfloat16).at[got_slots].set(got_rows, mode="drop")
-    group_both = lax.all_gather(relaid, MEMBER, axis=0, tiled=True)
+    group_both = lax.all_gather(relaid, ("core", "chip"), axis=0, tiled=True)
+    half = group_rows // 2
+    positive_member = positive // rows
+    positive = positive_member % 2 * half + positive_member // 2 * rows + positive % rows
     group_passages = group_both[:, :width]
     group_hidden = group_both[:, width:]
     scores = contract(query_emb, group_passages, 1, 1) * factor
@@ -78,9 +81,9 @@
         weight_share = weight_share + lax.ppermute(weight_share, "group", pairs)
         step *= 2
     grad_weight = lax.all_gather(weight_share / devices, MEMBER, axis=0, tiled=True)
-    split = partial.reshape(chips, 2, rows, width)
-    kept = jnp.where(core == 0, split[:, 0], split[:, 1])
-    given = jnp.where(core == 0, split[:, 1], split[:, 0]).astype(jnp.bfloat16)
+    kept = jnp.where(core == 0, partial[:half], partial[half:]).reshape(chips, rows, width)
+    given = lax.dynamic_slice_in_dim(partial, (1 - core) * half, half)
+    given = given.reshape(chips, rows, width).astype(jnp.bfloat16)
     paired = kept + lax.ppermute(given, "core", swap).astype(jnp.float32)
     pieces = lax.all_to_all(
         paired.astype(jnp.bfloat16), "chip", split_axis=0, concat_axis=0, tiled=True

time: 269 us -> 275 us (1.022)
  local copies, waits for them, and re-layouts: 11.7 us -> 16.4 us
    select_n x0 -> x1, other arithmetic: none -> 5.41 us  [body(): jnp.where(core == 0, partial[:half], partial[half:])]
    convert_element_type x0 -> x1, local copies, waits for them, and re-layouts: none -> 4.75 us  [body(): given = given.reshape(chips, rows, width).astype(jnp.bfloat16)]
    convert_element_type x1, other arithmetic: 8.52 us -> 4.68 us  [body(): paired.astype(jnp.bfloat16)]
  transfers between devices with their start and end apart: 8 -> 8, of which waited for: 6 -> 5; matrix products, arithmetic and copies ran while one was open for 8% -> 10% of each run, Pallas kernels for 0% -> 0%
where the time goes in v5:
time: 275 us
  waiting for transfers between devices  108 us (39%)
  blocking collectives  50.6 us (18%)
  matrix products  33.6 us (12%)
  other arithmetic  27.3 us (10%)
  starting transfers between devices  23.8 us (9%)
  local copies, waits for them, and re-layouts  16.4 us (6%)
  between operations  14.4 us (5%)
    all_gather x1, waiting for transfers between devices, body(): group_both = lax.all_gather(relaid, ('core', 'chip'), axis=0, tiled=True)  57.5 us
    all_to_all x1, waiting for transfers between devices, body(): lax.all_to_all(paired.astype(jnp.bfloat16), 'chip', split_axis=0, concat_...  36.2 us
    all_to_all x1, blocking collectives, body(): lax.all_to_all(send_rows, ALL, split_axis=0, concat_axis=0, tiled=True)  28.2 us
    all_to_all x1, blocking collectives, body(): weight_pieces = lax.all_to_all(weight_paired, 'chip', 0, 0, tiled=True)  22.3 us
    dot_general x6, matrix products, contract(): lax.dot_general(left, right, (((left_dim,), (right_dim,)), ((), ())), pre...  21.2 us
    all_to_all x1, starting transfers between devices, body(): lax.all_to_all(back_rows, ALL, split_axis=0, concat_axis=0, tiled=True)  14.4 us
    all_to_all x1, waiting for transfers between devices, body(): lax.all_to_all(back_rows, ALL, split_axis=0, concat_axis=0, tiled=True)  10.5 us
    dot_general x1, matrix products, body(): jnp.dot(coef, group_passages, preferred_element_type=jnp.float32)  9.27 us
  transfers between devices with their start and end apart: 8, of which 5 were waited for; matrix products, arithmetic and copies ran while one was open for 10% of the time, Pallas kernels for 0%

profile of v5, /device:TPU:1, one launch (start us, length us, event | category | flops | bytes accessed | tf_op | source)
XLA Modules:
  0.0 274.6 jit_solution(2525179772671832669)
XLA Ops:
  7.2 0.8 fusion.30
  8.0 0.7 and_select_fusion.1
  8.7 0.2 convert_reduce_fusion
  8.9 1.3 convolution_convert_fusion.3
  10.2 0.1 broadcast_in_dim.11
  10.3 0.1 scatter.22
  10.3 2.1 scatter_custom_fusion
  12.5 0.3 all_to_all.22
  12.8 28.2 %all_to_all.34 = bf16[128,2,1664]{2,1,0:T(2,128)(2,1)} all-to-all(bf16[128,2,1664]{2,1,0:T(2,128)(2,1)S(1)} %all_to_all.22), channel_id=1, replica_groups=mesh['group'=4,'chip'=16,'core'=2] {'group','chip','core'}, dimensions={0} | all-to-all | bytes 1703936 | tf_op jit(solution)/shard_map/all_to_all | solution.py:45
  41.1 2.4 all_to_all.24
  43.4 0.2 fusion.21
  43.6 2.5 scatter_custom_fusion.1
  46.2 1.9 convolution_convert_fusion.1
  48.1 57.5 %all-gather.3.cloned.1.call-done = bf16[4096,1536]{1,0:T(8,128)(2,1)} async-done(((bf16[128,1536]{1,0:T(8,128)(2,1)}), bf16[4096,1536]{1,0:T(8,128)(2,1)}) %all-gather.3.cloned.1.call-update) | async-done | bytes 12582928 | tf_op jit(solution)/shard_map/all_gather | solution.py:49
  105.6 5.8 %multiply_reduce_fusion = (f32[512]{0:T(512)S(1)}, f32[512,4096]{1,0:T(8,128)S(1)}) fusion(bf16[512,768]{1,0:T(8,128)(2,1)S(1)} %convolution_convert_fusion.1, bf16[4096,1536]{1,0:T(8,128)(2,1)} %all-gather.3.cloned.1.call-done), kind=kOutput, calls=%fused_computation.8 | convolution fusion | flops 3225419264 | bytes 15468544 | tf_op jit(solution)/shard_map/dot_general | solution.py:14
  111.5 3.1 %select_reduce_fusion = (f32[512]{0:T(512)S(1)}, f32[512]{0:T(512)S(1)}) fusion(f32[512,4096]{1,0:T(8,128)S(1)} %get-tuple-element.25, s32[512]{0:T(512)S(1)} %fusion.25, f32[512]{0:T(512)S(1)} %get-tuple-element.24), kind=kLoop, calls=%fused_computation.5 | loop fusion | flops 12581888 | bytes 8396800 | tf_op jit(solution)/shard_map/reduce_sum | solution.py:59
  114.6 0.6 fusion.31
  115.2 3.9 %multiply_convert_fusion = bf16[512,4096]{1,0:T(8,128)(2,1)S(1)} fusion(f32[512,4096]{1,0:T(8,128)S(1)} %get-tuple-element.25, f32[512]{0:T(512)S(1)} %get-tuple-element.21, f32[512]{0:T(512)S(1)} %copy-done.5, s32[512]{0:T(512)S(1)} %fusion.25), kind=kLoop, calls=%fused_computation.4 | loop fusion | flops 16777216 | bytes 12589056 | tf_op jit(solution)/shard_map/convert_element_type | solution.py:62
  119.1 3.6 %fusion.32 = f32[4096,768]{1,0:T(8,128)S(1)} fusion(bf16[512,4096]{1,0:T(8,128)(2,1)S(1)} %multiply_convert_fusion, bf16[512,768]{1,0:T(8,128)(2,1)S(1)} %convolution_convert_fusion.1), kind=kOutput, calls=%fused_computation.77 | convolution fusion | flops 3221225472 | bytes 17563648 | tf_op jit(solution)/shard_map/dot_general | solution.py:14
  122.7 9.3 %fusion.6 = bf16[512,768]{1,0:T(8,128)(2,1)S(1)} fusion(bf16[512,4096]{1,0:T(8,128)(2,1)S(1)} %multiply_convert_fusion, bf16[4096,1536]{1,0:T(8,128)(2,1)} %all-gather.3.cloned.1.call-done), kind=kOutput, calls=%fused_computation.21 | convolution fusion | flops 3221618688 | bytes 11272192 | tf_op jit(solution)/shard_map/dot_general | solution.py:63
  132.0 8.0 %fusion = f32[768,768]{1,0:T(8,128)S(1)} fusion(f32[4096,768]{1,0:T(8,128)S(1)} %fusion.32, bf16[4096,1536]{1,0:T(8,128)(2,1)} %all-gather.3.cloned.1.call-done), kind=kOutput, calls=%fused_computation.9 | convolution fusion | flops 4831838208 | bytes 21233664 | tf_op jit(solution)/shard_map/dot_general | solution.py:14
  140.0 0.9 bitcast_add_fusion
  140.9 1.1 select_bitcast_fusion
  142.0 0.3 collective-permute-start.1
  142.3 4.8 %dynamic-slice_convert_fusion = bf16[2048,768]{1,0:T(8,128)(2,1)} fusion(f32[4096,768]{1,0:T(8,128)} %copy-done.1, s32[]{:T(128)S(6)} %select_n.86), kind=kLoop, calls=%fused_computation.13 | loop fusion | bytes 6291460 | tf_op jit(solution)/shard_map/convert_element_type | solution.py:86
  147.0 0.3 collective-permute-start
  147.3 1.5 fusion.10
  148.8 22.3 %all_to_all.35 = f32[16,24,768]{2,1,0:T(8,128)S(1)} all-to-all(f32[16,24,768]{2,1,0:T(8,128)S(1)} %fusion.10), channel_id=1, replica_groups=mesh['group'=4,'chip'=16,'core'=2] {'chip'}, dimensions={0} | all-to-all | bytes 2359296 | tf_op jit(solution)/shard_map/all_to_all | solution.py:76
  171.1 0.1 reduce_sum.52
  171.2 1.4 collective-permute-start.2
  172.6 1.9 collective-permute-done.2
  174.5 3.0 %collective-permute-start.3 = (f32[24,768]{1,0:T(8,128)S(1)}, f32[24,768]{1,0:T(8,128)S(1)}, u32[]{:S(2)}, u32[]{:S(2)}) collective-permute-start(f32[24,768]{1,0:T(8,128)S(1)} %add.87), channel_id=1, source_target_pairs={{0,64},{32,96},{64,0},{96,32},{1,65},{33,97},{65,1},{97,33},{2,66}... | collective-permute-start | bytes 221192 | tf_op jit(solution)/shard_map/ppermute | solution.py:81
  177.5 2.3 collective-permute-done.3
  179.7 0.6 add_multiply_fusion
  180.4 5.4 %slice_select_fusion = f32[2048,768]{1,0:T(8,128)S(1)} fusion(f32[4096,768]{1,0:T(8,128)} %copy-done.1, pred[]{:T(512)S(6)} %eq.42), kind=kLoop, calls=%fused_computation.11 | loop fusion | flops 1572864 | bytes 18874368 | tf_op jit(solution)/shard_map/jit(_where)/select_n | solution.py:84
  185.8 4.7 %add_convert_fusion = bf16[16,128,768]{2,1,0:T(8,128)(2,1)} fusion(f32[16,128,768]{2,1,0:T(8,128)S(1)} %bitcast.40, bf16[16,128,768]{2,1,0:T(8,128)(2,1)} %collective-permute-done), kind=kLoop, calls=%fused_computation.12 | loop fusion | flops 4718592 | bytes 12582912 | tf_op jit(solution)/shard_map/convert_element_type | solution.py:89
  190.5 4.5 %all-to-all-start.1 = ((bf16[16,128,768]{2,1,0:T(8,128)(2,1)}), bf16[16,128,768]{2,1,0:T(8,128)(2,1)}, u32[]{:S(2)}, u32[]{:S(2)}) async-start(bf16[16,128,768]{2,1,0:T(8,128)(2,1)} %add_convert_fusion), calls=%async_computation.1 | async-start | bytes 6291456 | tf_op jit(solution)/shard_map/all_to_all | solution.py:88
  195.0 36.2 %all-to-all-done.1 = bf16[16,128,768]{2,1,0:T(8,128)(2,1)} async-done(((bf16[16,128,768]{2,1,0:T(8,128)(2,1)}), bf16[16,128,768]{2,1,0:T(8,128)(2,1)}, u32[]{:S(2)}, u32[]{:S(2)}) %all-to-all-start.1) | async-done | bytes 3145760 | tf_op jit(solution)/shard_map/all_to_all | solution.py:88
  231.3 2.3 reduce_sum.51
  233.6 1.2 gather_fusion
  234.8 0.9 all_to_all.26
  235.7 14.4 %all-to-all-start.2 = ((bf16[128,2,768]{2,1,0:T(2,128)(2,1)}), bf16[128,2,768]{2,1,0:T(2,128)(2,1)S(1)}, u32[]{:S(2)}, u32[]{:S(2)}) async-start(bf16[128,2,768]{2,1,0:T(2,128)(2,1)} %all_to_all.26), calls=%async_computation.2 | async-start | bytes 786432 | tf_op jit(solution)/shard_map/all_to_all | solution.py:93
  250.1 1.7 convolution_convert_fusion
  251.8 10.5 %all-to-all-done.2 = bf16[128,2,768]{2,1,0:T(2,128)(2,1)S(1)} async-done(((bf16[128,2,768]{2,1,0:T(2,128)(2,1)}), bf16[128,2,768]{2,1,0:T(2,128)(2,1)S(1)}, u32[]{:S(2)}, u32[]{:S(2)}) %all-to-all-start.2) | async-done | bytes 393248 | tf_op jit(solution)/shard_map/all_to_all | solution.py:93
  262.2 0.1 all_to_all.28
  262.4 0.9 gather_fusion.1
  263.3 1.2 convolution_convert_fusion.2
  264.5 3.2 %copy.30 = f32[768,768]{1,0:T(8,128)} copy(f32[768,768]{1,0:T(8,128)} %all-gather.5.cloned.1.call-done) | data formatting | bytes 4718592
  (28 shorter events, 0.2 us)
Async XLA Ops:
  7.2 1.7 copy-start
  7.2 98.5 %all-gather.3.cloned.1.call-start = ((), (), s32[]{:S(2)}) async-start(), calls=%async_computation.4 | async-start | bytes 12976128 | tf_op jit(solution)/shard_map/all_gather | solution.py:49
  10.3 35.8 %copy-start.6 = (s32[512]{0:T(512)S(1)}, s32[512]{0:T(512)}, u32[]{:S(2)}) copy-start(s32[512]{0:T(512)} %param.14) | copy-start | bytes 6148
  46.1 218.4 %all-gather.5.cloned.1.call-start = ((), (), s32[]{:S(2)}) async-start(), calls=%async_computation.5 | async-start | bytes 2433024 | tf_op jit(solution)/shard_map/all_gather | solution.py:83
  111.5 3.7 %copy-start.5 = (f32[512]{0:T(512)S(1)}, f32[512]{0:T(512)}, u32[]{:S(2)}) copy-start(f32[512]{0:T(512)} %param.15) | copy-start | bytes 6148
  122.7 9.3 %copy-start.1 = (f32[4096,768]{1,0:T(8,128)}, f32[4096,768]{1,0:T(8,128)S(1)}, u32[]{:S(2)}) copy-start(f32[4096,768]{1,0:T(8,128)S(1)} %fusion.32) | copy-start | bytes 37748740
  132.0 8.0 %copy-start.3 = (bf16[512,768]{1,0:T(8,128)(2,1)}, bf16[512,768]{1,0:T(8,128)(2,1)S(1)}, u32[]{:S(2)}) copy-start(bf16[512,768]{1,0:T(8,128)(2,1)S(1)} %fusion.6) | copy-start | bytes 2359300
  132.0 8.0 %copy-start.2 = (bf16[512,768]{1,0:T(8,128)(2,1)S(1)}, bf16[512,768]{1,0:T(8,128)(2,1)}, u32[]{:S(2)}) copy-start(bf16[512,768]{1,0:T(8,128)(2,1)} %param.10) | copy-start | bytes 2359300
  142.0 5.3 %collective-permute-start.1 = (f32[16,24,768]{2,1,0:T(8,128)}, f32[16,24,768]{2,1,0:T(8,128)}, u32[]{:S(2)}, u32[]{:S(2)}) collective-permute-start(f32[16,24,768]{2,1,0:T(8,128)} %select_bitcast_fusion), channel_id=1, source_target_pairs={{0,1},{1,0},{2,3},{3,2},{4,5},{5,4},{6,7},{7,6},{8,9},{9,8},{10,11... | collective-permute-start | bytes 3538952 | tf_op jit(solution)/shard_map/ppermute | solution.py:75
  147.0 38.8 %collective-permute-start = (bf16[16,128,768]{2,1,0:T(8,128)(2,1)}, bf16[16,128,768]{2,1,0:T(8,128)(2,1)}, u32[]{:S(2)}, u32[]{:S(2)}) collective-permute-start(bf16[16,128,768]{2,1,0:T(8,128)(2,1)} %bitcast.1), channel_id=1, source_target_pairs={{0,1},{1,0},{2,3},{3,2},{4,5},{5,4},{6,7},{7,6},{8,9},{9,8},{10,11... | collective-permute-start | bytes 9437192 | tf_op jit(solution)/shard_map/ppermute | solution.py:87
  171.2 3.3 %collective-permute-start.2 = (f32[24,768]{1,0:T(8,128)S(1)}, f32[24,768]{1,0:T(8,128)S(1)}, u32[]{:S(2)}, u32[]{:S(2)}) collective-permute-start(f32[24,768]{1,0:T(8,128)S(1)} %reduce_sum.52), channel_id=1, source_target_pairs={{0,32},{32,0},{64,96},{96,64},{1,33},{33,1},{65,97},{97,65},{2,34}... | collective-permute-start | bytes 221192 | tf_op jit(solution)/shard_map/ppermute | solution.py:81
  174.5 5.2 %collective-permute-start.3 = (f32[24,768]{1,0:T(8,128)S(1)}, f32[24,768]{1,0:T(8,128)S(1)}, u32[]{:S(2)}, u32[]{:S(2)}) collective-permute-start(f32[24,768]{1,0:T(8,128)S(1)} %add.87), channel_id=1, source_target_pairs={{0,64},{32,96},{64,0},{96,32},{1,65},{33,97},{65,1},{97,33},{2,66}... | collective-permute-start | bytes 221192 | tf_op jit(solution)/shard_map/ppermute | solution.py:81
  190.5 40.8 %all-to-all-start.1 = ((bf16[16,128,768]{2,1,0:T(8,128)(2,1)}), bf16[16,128,768]{2,1,0:T(8,128)(2,1)}, u32[]{:S(2)}, u32[]{:S(2)}) async-start(bf16[16,128,768]{2,1,0:T(8,128)(2,1)} %add_convert_fusion), calls=%async_computation.1 | async-start | bytes 6291456 | tf_op jit(solution)/shard_map/all_to_all | solution.py:88
  195.0 55.1 %copy-start.4 = (bf16[512,768]{1,0:T(8,128)(2,1)S(1)}, bf16[512,768]{1,0:T(8,128)(2,1)}, u32[]{:S(2)}) copy-start(bf16[512,768]{1,0:T(8,128)(2,1)} %copy-done.3) | copy-start | bytes 2359300
  235.7 26.6 %all-to-all-start.2 = ((bf16[128,2,768]{2,1,0:T(2,128)(2,1)}), bf16[128,2,768]{2,1,0:T(2,128)(2,1)S(1)}, u32[]{:S(2)}, u32[]{:S(2)}) async-start(bf16[128,2,768]{2,1,0:T(2,128)(2,1)} %all_to_all.26), calls=%async_computation.2 | async-start | bytes 786432 | tf_op jit(solution)/shard_map/all_to_all | solution.py:93
Sparse Core Ops, SparseCore 0:
  46.2 59.3 all-gather.2
  180.5 68.2 all-gather.4

commit v6 on v5

--- a/solution.py
+++ b/solution.py
@@ -6,7 +6,6 @@
 from jax.sharding import PartitionSpec as P
 
 
-MEMBER = ("chip", "core")
 ALL = ("group", "chip", "core")
 
 
@@ -69,9 +68,9 @@
     chips = lax.axis_size("chip")
     core = lax.axis_index("core")
     swap = [(0, 1), (1, 0)]
-    weight_split = local_weight.reshape(chips, 2, weight_rows, width)
-    weight_kept = jnp.where(core == 0, weight_split[:, 0], weight_split[:, 1])
-    weight_given = jnp.where(core == 0, weight_split[:, 1], weight_split[:, 0])
+    weight_split = local_weight.reshape(2, chips, weight_rows, width)
+    weight_kept = jnp.where(core == 0, weight_split[0], weight_split[1])
+    weight_given = jnp.where(core == 0, weight_split[1], weight_split[0])
     weight_paired = weight_kept + lax.ppermute(weight_given, "core", swap)
     weight_pieces = lax.all_to_all(weight_paired, "chip", 0, 0, tiled=True)
     weight_share = jnp.sum(weight_pieces, axis=0)
@@ -80,8 +79,8 @@
         pairs = [(index, index ^ step) for index in range(groups)]
         weight_share = weight_share + lax.ppermute(weight_share, "group", pairs)
         step *= 2
-    grad_weight = lax.all_gather(weight_share / devices, MEMBER, axis=0, tiled=True)
-    kept = jnp.where(core == 0, partial[:half], partial[half:]).reshape(chips, rows, width)
+    grad_weight = lax.all_gather(weight_share / devices, ("core", "chip"), axis=0, tiled=True)
+    kept = lax.dynamic_slice_in_dim(partial, core * half, half).reshape(chips, rows, width)
     given = lax.dynamic_slice_in_dim(partial, (1 - core) * half, half)
     given = given.reshape(chips, rows, width).astype(jnp.bfloat16)
     paired = kept + lax.ppermute(given, "core", swap).astype(jnp.float32)

time: 275 us -> 269 us (0.978)
  other arithmetic: 27.3 us -> 19.2 us
  waiting for transfers between devices: 108 us -> 111 us
    select_n x2 -> x1, other arithmetic: 6.55 us -> 0.16 us  [body(): weight_given = jnp.where(core == 0, weight_split[1], weight_split[0])]
    dynamic_slice x0 -> x1, local copies, waits for them, and re-layouts: none -> 3.19 us  [body(): lax.dynamic_slice_in_dim(partial, core * half, half)]
  transfers between devices with their start and end apart: 8 -> 8, of which waited for: 5 -> 6; matrix products, arithmetic and copies ran while one was open for 10% -> 13% of each run, Pallas kernels for 0% -> 0%
where the time goes in v6:
time: 269 us; the launch traced here: 268 us
  waiting for transfers between devices  111 us (41%)
  blocking collectives  50.6 us (19%)
  matrix products  31.9 us (12%)
  starting transfers between devices  23.6 us (9%)
  other arithmetic  19.2 us (7%)
  local copies, waits for them, and re-layouts  17.2 us (6%)
  between operations  14.3 us (5%)
    all_gather x1, waiting for transfers between devices, body(): group_both = lax.all_gather(relaid, ('core', 'chip'), axis=0, tiled=True)  57.4 us
    all_to_all x1, waiting for transfers between devices, body(): lax.all_to_all(paired.astype(jnp.bfloat16), 'chip', split_axis=0, concat_...  36.8 us
    all_to_all x1, blocking collectives, body(): lax.all_to_all(send_rows, ALL, split_axis=0, concat_axis=0, tiled=True)  28.2 us
    all_to_all x1, blocking collectives, body(): weight_pieces = lax.all_to_all(weight_paired, 'chip', 0, 0, tiled=True)  22.4 us
    dot_general x6, matrix products, contract(): lax.dot_general(left, right, (((left_dim,), (right_dim,)), ((), ())), pre...  20.8 us
    all_to_all x1, starting transfers between devices, body(): lax.all_to_all(back_rows, ALL, split_axis=0, concat_axis=0, tiled=True)  13.9 us
    all_to_all x1, waiting for transfers between devices, body(): lax.all_to_all(back_rows, ALL, split_axis=0, concat_axis=0, tiled=True)  10.5 us
    dot_general x1, matrix products, body(): jnp.dot(coef, group_passages, preferred_element_type=jnp.float32)  7.96 us
  transfers between devices with their start and end apart: 8, of which 6 were waited for; matrix products, arithmetic and copies ran while one was open for 13% of the time, Pallas kernels for 0%

profile of v6, /device:TPU:1, one launch (start us, length us, event | category | flops | bytes accessed | tf_op | source)
XLA Modules:
  0.0 268.3 jit_solution(14177239602280990459)
XLA Ops:
  7.2 0.8 fusion.28
  8.0 0.7 and_select_fusion.1
  8.7 0.2 convert_reduce_fusion
  8.9 1.3 convolution_convert_fusion.3
  10.2 0.1 broadcast_in_dim.11
  10.3 2.1 scatter_custom_fusion
  12.5 0.3 all_to_all.22
  12.8 28.2 %all_to_all.34 = bf16[128,2,1664]{2,1,0:T(2,128)(2,1)} all-to-all(bf16[128,2,1664]{2,1,0:T(2,128)(2,1)S(1)} %all_to_all.22), channel_id=1, replica_groups=mesh['group'=4,'chip'=16,'core'=2] {'group','chip','core'}, dimensions={0} | all-to-all | bytes 1703936 | tf_op jit(solution)/shard_map/all_to_all | solution.py:44
  41.1 2.4 all_to_all.24
  43.4 0.2 fusion.19
  43.6 2.5 scatter_custom_fusion.1
  46.1 0.2 all-gather.5.cloned.1.call-start
  46.4 1.9 convolution_convert_fusion.1
  48.3 57.4 %all-gather.3.cloned.1.call-done = bf16[4096,1536]{1,0:T(8,128)(2,1)} async-done(((bf16[128,1536]{1,0:T(8,128)(2,1)}), bf16[4096,1536]{1,0:T(8,128)(2,1)}) %all-gather.3.cloned.1.call-update) | async-done | bytes 12582928 | tf_op jit(solution)/shard_map/all_gather | solution.py:48
  105.6 5.8 %multiply_reduce_fusion = (f32[512]{0:T(512)S(1)}, f32[512,4096]{1,0:T(8,128)S(1)}) fusion(bf16[512,768]{1,0:T(8,128)(2,1)S(1)} %convolution_convert_fusion.1, bf16[4096,1536]{1,0:T(8,128)(2,1)} %all-gather.3.cloned.1.call-done), kind=kOutput, calls=%fused_computation.8 | convolution fusion | flops 3225419264 | bytes 15468544 | tf_op jit(solution)/shard_map/dot_general | solution.py:13
  111.5 3.1 %select_reduce_fusion = (f32[512]{0:T(512)S(1)}, f32[512]{0:T(512)S(1)}) fusion(f32[512,4096]{1,0:T(8,128)S(1)} %get-tuple-element.27, s32[512]{0:T(512)S(1)} %fusion.23, f32[512]{0:T(512)S(1)} %get-tuple-element.26), kind=kLoop, calls=%fused_computation.5 | loop fusion | flops 12581888 | bytes 8396800 | tf_op jit(solution)/shard_map/reduce_sum | solution.py:58
  114.6 0.6 fusion.29
  115.1 3.9 %multiply_convert_fusion = bf16[512,4096]{1,0:T(8,128)(2,1)S(1)} fusion(f32[512,4096]{1,0:T(8,128)S(1)} %get-tuple-element.27, f32[512]{0:T(512)S(1)} %get-tuple-element.21, f32[512]{0:T(512)S(1)} %copy-done.3, s32[512]{0:T(512)S(1)} %fusion.23), kind=kLoop, calls=%fused_computation.4 | loop fusion | flops 16777216 | bytes 12589056 | tf_op jit(solution)/shard_map/convert_element_type | solution.py:61
  119.0 3.6 %fusion.30 = f32[4096,768]{1,0:T(8,128)S(1)} fusion(bf16[512,4096]{1,0:T(8,128)(2,1)S(1)} %multiply_convert_fusion, bf16[512,768]{1,0:T(8,128)(2,1)S(1)} %convolution_convert_fusion.1), kind=kOutput, calls=%fused_computation.75 | convolution fusion | flops 3221225472 | bytes 17563648 | tf_op jit(solution)/shard_map/dot_general | solution.py:13
  122.6 2.3 dynamic-slice_convert_fusion
  125.0 0.3 collective-permute-start
  125.2 8.0 %fusion.6 = bf16[512,768]{1,0:T(8,128)(2,1)S(1)} fusion(bf16[512,4096]{1,0:T(8,128)(2,1)S(1)} %multiply_convert_fusion, bf16[4096,1536]{1,0:T(8,128)(2,1)} %all-gather.3.cloned.1.call-done), kind=kOutput, calls=%fused_computation.20 | convolution fusion | flops 3221618688 | bytes 11272192 | tf_op jit(solution)/shard_map/dot_general | solution.py:62
  133.2 7.6 %fusion = f32[768,768]{1,0:T(8,128)S(1)} fusion(f32[4096,768]{1,0:T(8,128)S(1)} %fusion.30, bf16[4096,1536]{1,0:T(8,128)(2,1)} %all-gather.3.cloned.1.call-done), kind=kOutput, calls=%fused_computation.9 | convolution fusion | flops 4831838208 | bytes 21233664 | tf_op jit(solution)/shard_map/dot_general | solution.py:13
  140.9 0.9 bitcast_add_fusion
  141.8 0.2 slice_select_fusion
  141.9 0.3 collective-permute-start.1
  142.3 2.6 collective-permute-done.1
  144.9 0.1 add.90
  145.0 22.4 %all_to_all.35 = f32[16,24,768]{2,1,0:T(8,128)S(1)} all-to-all(f32[16,24,768]{2,1,0:T(8,128)S(1)} %add.90), channel_id=1, replica_groups=mesh['group'=4,'chip'=16,'core'=2] {'chip'}, dimensions={0} | all-to-all | bytes 2359296 | tf_op jit(solution)/shard_map/all_to_all | solution.py:75
  167.4 1.4 collective-permute-start.2
  168.8 1.9 collective-permute-done.2
  170.7 3.0 %collective-permute-start.3 = (f32[24,768]{1,0:T(8,128)S(1)}, f32[24,768]{1,0:T(8,128)S(1)}, u32[]{:S(2)}, u32[]{:S(2)}) collective-permute-start(f32[24,768]{1,0:T(8,128)S(1)} %add.91), channel_id=1, source_target_pairs={{0,64},{32,96},{64,0},{96,32},{1,65},{33,97},{65,1},{97,33},{2,66}... | collective-permute-start | bytes 221192 | tf_op jit(solution)/shard_map/ppermute | solution.py:80
  173.7 2.3 collective-permute-done.3
  175.9 0.6 add_multiply_fusion
  176.6 3.2 %constant_dynamic-slice_fusion = f32[2048,768]{1,0:T(8,128)S(1)} fusion(f32[4096,768]{1,0:T(8,128)} %copy-done.1, s32[]{:T(128)S(6)} %select_n.79), kind=kLoop, calls=%fused_computation.72 | loop fusion | bytes 12582916 | tf_op jit(solution)/shard_map/dynamic_slice | solution.py:83
  179.8 4.4 %add_convert_fusion = bf16[16,128,768]{2,1,0:T(8,128)(2,1)} fusion(f32[16,128,768]{2,1,0:T(8,128)S(1)} %bitcast.23, bf16[16,128,768]{2,1,0:T(8,128)(2,1)} %collective-permute-done), kind=kLoop, calls=%fused_computation.11 | loop fusion | flops 4718592 | bytes 12582912 | tf_op jit(solution)/shard_map/convert_element_type | solution.py:88
  184.2 4.5 %all-to-all-start.1 = ((bf16[16,128,768]{2,1,0:T(8,128)(2,1)}), bf16[16,128,768]{2,1,0:T(8,128)(2,1)}, u32[]{:S(2)}, u32[]{:S(2)}) async-start(bf16[16,128,768]{2,1,0:T(8,128)(2,1)} %add_convert_fusion), calls=%async_computation.1 | async-start | bytes 6291456 | tf_op jit(solution)/shard_map/all_to_all | solution.py:87
  188.7 36.8 %all-to-all-done.1 = bf16[16,128,768]{2,1,0:T(8,128)(2,1)} async-done(((bf16[16,128,768]{2,1,0:T(8,128)(2,1)}), bf16[16,128,768]{2,1,0:T(8,128)(2,1)}, u32[]{:S(2)}, u32[]{:S(2)}) %all-to-all-start.1) | async-done | bytes 3145760 | tf_op jit(solution)/shard_map/all_to_all | solution.py:87
  225.5 2.3 reduce_sum.51
  227.8 1.2 gather_fusion
  229.0 0.9 all_to_all.26
  229.9 13.9 %all-to-all-start.2 = ((bf16[128,2,768]{2,1,0:T(2,128)(2,1)}), bf16[128,2,768]{2,1,0:T(2,128)(2,1)S(1)}, u32[]{:S(2)}, u32[]{:S(2)}) async-start(bf16[128,2,768]{2,1,0:T(2,128)(2,1)} %all_to_all.26), calls=%async_computation.2 | async-start | bytes 786432 | tf_op jit(solution)/shard_map/all_to_all | solution.py:92
  243.9 1.7 convolution_convert_fusion
  245.6 10.5 %all-to-all-done.2 = bf16[128,2,768]{2,1,0:T(2,128)(2,1)S(1)} async-done(((bf16[128,2,768]{2,1,0:T(2,128)(2,1)}), bf16[128,2,768]{2,1,0:T(2,128)(2,1)S(1)}, u32[]{:S(2)}, u32[]{:S(2)}) %all-to-all-start.2) | async-done | bytes 393248 | tf_op jit(solution)/shard_map/all_to_all | solution.py:92
  256.0 0.1 all_to_all.28
  256.2 0.9 gather_fusion.1
  257.0 1.2 convolution_convert_fusion.2
  258.3 3.2 %copy.13 = f32[768,768]{1,0:T(8,128)} copy(f32[768,768]{1,0:T(8,128)} %all-gather.5.cloned.1.call-done) | data formatting | bytes 4718592
  (24 shorter events, 0.3 us)
Async XLA Ops:
  7.2 1.7 copy-start
  7.2 39.1 %copy-start.4 = (s32[512]{0:T(512)S(1)}, s32[512]{0:T(512)}, u32[]{:S(2)}) copy-start(s32[512]{0:T(512)} %param.14) | copy-start | bytes 6148
  7.2 98.4 %all-gather.3.cloned.1.call-start = ((), (), s32[]{:S(2)}) async-start(), calls=%async_computation.4 | async-start | bytes 12976128 | tf_op jit(solution)/shard_map/all_gather | solution.py:48
  46.1 212.2 %all-gather.5.cloned.1.call-start = ((), (), s32[]{:S(2)}) async-start(), calls=%async_computation.5 | async-start | bytes 2433024 | tf_op jit(solution)/shard_map/all_gather | solution.py:82
  111.4 3.7 %copy-start.3 = (f32[512]{0:T(512)S(1)}, f32[512]{0:T(512)}, u32[]{:S(2)}) copy-start(f32[512]{0:T(512)} %param.15) | copy-start | bytes 6148
  122.6 10.6 %copy-start.1 = (f32[4096,768]{1,0:T(8,128)}, f32[4096,768]{1,0:T(8,128)S(1)}, u32[]{:S(2)}) copy-start(f32[4096,768]{1,0:T(8,128)S(1)} %fusion.30) | copy-start | bytes 37748740
  125.0 54.8 %collective-permute-start = (bf16[16,128,768]{2,1,0:T(8,128)(2,1)}, bf16[16,128,768]{2,1,0:T(8,128)(2,1)}, u32[]{:S(2)}, u32[]{:S(2)}) collective-permute-start(bf16[16,128,768]{2,1,0:T(8,128)(2,1)} %bitcast.1), channel_id=1, source_target_pairs={{0,1},{1,0},{2,3},{3,2},{4,5},{5,4},{6,7},{7,6},{8,9},{9,8},{10,11... | collective-permute-start | bytes 9437192 | tf_op jit(solution)/shard_map/ppermute | solution.py:86
  133.2 7.7 %copy-start.2 = (bf16[512,768]{1,0:T(8,128)(2,1)S(1)}, bf16[512,768]{1,0:T(8,128)(2,1)}, u32[]{:S(2)}) copy-start(bf16[512,768]{1,0:T(8,128)(2,1)} %param.10) | copy-start | bytes 2359300
  141.9 2.9 %collective-permute-start.1 = (f32[16,24,768]{2,1,0:T(8,128)S(1)}, f32[16,24,768]{2,1,0:T(8,128)S(1)}, u32[]{:S(2)}, u32[]{:S(2)}) collective-permute-start(f32[16,24,768]{2,1,0:T(8,128)S(1)} %bitcast.25), channel_id=1, source_target_pairs={{0,1},{1,0},{2,3},{3,2},{4,5},{5,4},{6,7},{7,6},{8,9},{9,8},{10,11... | collective-permute-start | bytes 3538952 | tf_op jit(solution)/shard_map/ppermute | solution.py:74
  167.4 3.3 %collective-permute-start.2 = (f32[24,768]{1,0:T(8,128)S(1)}, f32[24,768]{1,0:T(8,128)S(1)}, u32[]{:S(2)}, u32[]{:S(2)}) collective-permute-start(f32[24,768]{1,0:T(8,128)S(1)} %reduce_sum.52), channel_id=1, source_target_pairs={{0,32},{32,0},{64,96},{96,64},{1,33},{33,1},{65,97},{97,65},{2,34}... | collective-permute-start | bytes 221192 | tf_op jit(solution)/shard_map/ppermute | solution.py:80
  170.7 5.2 %collective-permute-start.3 = (f32[24,768]{1,0:T(8,128)S(1)}, f32[24,768]{1,0:T(8,128)S(1)}, u32[]{:S(2)}, u32[]{:S(2)}) collective-permute-start(f32[24,768]{1,0:T(8,128)S(1)} %add.91), channel_id=1, source_target_pairs={{0,64},{32,96},{64,0},{96,32},{1,65},{33,97},{65,1},{97,33},{2,66}... | collective-permute-start | bytes 221192 | tf_op jit(solution)/shard_map/ppermute | solution.py:80
  184.2 41.3 %all-to-all-start.1 = ((bf16[16,128,768]{2,1,0:T(8,128)(2,1)}), bf16[16,128,768]{2,1,0:T(8,128)(2,1)}, u32[]{:S(2)}, u32[]{:S(2)}) async-start(bf16[16,128,768]{2,1,0:T(8,128)(2,1)} %add_convert_fusion), calls=%async_computation.1 | async-start | bytes 6291456 | tf_op jit(solution)/shard_map/all_to_all | solution.py:87
  229.9 26.1 %all-to-all-start.2 = ((bf16[128,2,768]{2,1,0:T(2,128)(2,1)}), bf16[128,2,768]{2,1,0:T(2,128)(2,1)S(1)}, u32[]{:S(2)}, u32[]{:S(2)}) async-start(bf16[128,2,768]{2,1,0:T(2,128)(2,1)} %all_to_all.26), calls=%async_computation.2 | async-start | bytes 786432 | tf_op jit(solution)/shard_map/all_to_all | solution.py:92
Sparse Core Ops, SparseCore 0:
  46.2 59.3 all-gather.2
  176.7 66.1 all-gather.4
